TPU v7x, 128 devices: a whole 4x4x4 slice. The times are simulated.
128 devices in a mesh: dp: 16 (over z_hi, x, core), tensor: 8 (over y, z_lo).
Axes of the slice: x: 4, y: 4, z: 4 (z_hi: 2, z_lo: 2; z = z_hi * 2 + z_lo), core: 2. Of those that a mesh axis runs over, the one named last changes fastest.
Arguments:
- layer_input: bfloat16 [16, 1024, 4096], P('dp', 'tensor'), may hold values from -9 to 9
- norm_gain: bfloat16 [4096], replicated, may hold values from 0.5 to 1.5
- w_query: bfloat16 [4096, 2048], P(None, 'tensor'), may hold values from -0.125 to 0.125
- w_key: bfloat16 [4096, 1024], P(None, 'tensor'), may hold values from -0.125 to 0.125
- value_weight: bfloat16 [4096, 1024], P(None, 'tensor'), may hold values from -0.09375 to 0.09375
- w_out: bfloat16 [2048, 4096], P('tensor'), may hold values from -0.125 to 0.125
- prefix_len: int32 [16], P('dp'), may hold values from 128 to 511
- grad_output: bfloat16 [16, 1024, 4096], P('dp', 'tensor'), may hold values from -6 to 6
Outputs:
- layer_output: bfloat16 [16, 1024, 4096], P('dp', 'tensor')
- grad_input: bfloat16 [16, 1024, 4096], P('dp', 'tensor')
- grad_gain: float32 [4096], replicated
- grad_query: bfloat16 [4096, 2048], P('dp', 'tensor')
- grad_key: bfloat16 [4096, 1024], P('dp', 'tensor')
- grad_value: bfloat16 [4096, 1024], P('dp', 'tensor')
- grad_wout: bfloat16 [2048, 4096], P('tensor', 'dp')
Inputs may be any that keep to these rules, and one draw needn't show every extreme that they name: `prefix_len`: the number of leading spectrum positions of each replica's sequence that every position attends to.
All inputs are finite; a program needn't handle non-finite values.
Results may differ from a plain program's by a relative error of at most 0.015.
The roundings to bfloat16 on the way count: a program that leaves them out, or rounds other values in their place, can miss the bound.
Values may be sent and summed in bfloat16 or wider, within the bound.
No kernel may reach another device: no remote copies, remote signals or barrier semaphores. Data moves between devices by JAX's collectives and lax.ppermute only.
A program may use at most 192 MiB of HBM per device.

v0:
```python
import jax
import jax.numpy as jnp
from jax import lax
from jax.sharding import PartitionSpec as P

HEAD_SIZE = 128


EPS = 1e-05


def convert_float(value):
    return value.astype(jnp.float32)


def per_device(
    layer_input, norm_gain, w_query, w_key, value_weight, w_out, prefix_len, grad_output
):
    heads_q = w_query.shape[1] // HEAD_SIZE
    heads_kv = w_key.shape[1] // HEAD_SIZE
    heads_per_group = heads_q // heads_kv
    scale_f = 1.0 / HEAD_SIZE**0.5
    rows_f = convert_float(layer_input[0])
    gain_vec = convert_float(norm_gain)
    inv_rms = lax.rsqrt(jnp.mean(rows_f * rows_f, axis=1, keepdims=True) + EPS)
    unit_rows = rows_f * inv_rms
    normed = (unit_rows * gain_vec).astype(jnp.bfloat16)
    full_normed = lax.all_gather(normed, "tensor", axis=0, tiled=True)
    sequence_length = full_normed.shape[0]
    query_matrix = jnp.dot(full_normed, w_query, preferred_element_type=jnp.float32).astype(
        jnp.bfloat16
    )
    key_projected = jnp.dot(full_normed, w_key, preferred_element_type=jnp.float32).astype(
        jnp.bfloat16
    )
    value_projected = jnp.dot(full_normed, value_weight, preferred_element_type=jnp.float32).astype(
        jnp.bfloat16
    )
    query_head_rows = query_matrix.reshape(sequence_length, heads_kv, heads_per_group, HEAD_SIZE)
    key_head_rows = key_projected.reshape(sequence_length, heads_kv, HEAD_SIZE)
    value_head_rows = value_projected.reshape(sequence_length, heads_kv, HEAD_SIZE)
    positions = lax.iota(jnp.int32, sequence_length)
    allowed = (positions[None, :] <= positions[:, None]) | (positions[None, :] < prefix_len[0])
    scores = (
        jnp.einsum(
            "skgd,tkd->kgst", query_head_rows, key_head_rows, preferred_element_type=jnp.float32
        )
        * scale_f
    )
    masked = jnp.where(allowed, scores, -1e30)
    row_max = jnp.max(masked, axis=-1, keepdims=True)
    expo_vals = jnp.exp(masked - row_max)
    attn_probs = expo_vals / jnp.sum(expo_vals, axis=-1, keepdims=True)
    probability_batch = attn_probs.astype(jnp.bfloat16)
    context = (
        jnp.einsum(
            "kgst,tkd->skgd", probability_batch, value_head_rows, preferred_element_type=jnp.float32
        )
        .astype(jnp.bfloat16)
        .reshape(sequence_length, heads_q * HEAD_SIZE)
    )
    product = jnp.dot(context, w_out, preferred_element_type=jnp.float32)
    attn_sum = lax.psum_scatter(
        convert_float(product.astype(jnp.bfloat16)).astype(jnp.bfloat16),
        "tensor",
        scatter_dimension=0,
        tiled=True,
    ).astype(jnp.float32)
    layer_output = (rows_f + attn_sum).astype(jnp.bfloat16)[None]
    grad_local = grad_output[0]
    full_grad = lax.all_gather(grad_local, "tensor", axis=0, tiled=True)
    context_gradient = jnp.einsum(
        "sd,hd->sh", full_grad, w_out, preferred_element_type=jnp.float32
    ).astype(jnp.bfloat16)
    wout_term = convert_float(
        jnp.einsum("sh,sd->hd", context, full_grad, preferred_element_type=jnp.float32).astype(
            jnp.bfloat16
        )
    )
    context_head_gradient = context_gradient.reshape(
        sequence_length, heads_kv, heads_per_group, HEAD_SIZE
    )
    d_probs = jnp.einsum(
        "skgd,tkd->kgst", context_head_gradient, value_head_rows, preferred_element_type=jnp.float32
    )
    row_delta = jnp.sum(d_probs * attn_probs, axis=-1, keepdims=True)
    scores_gradient = (attn_probs * (d_probs - row_delta) * scale_f).astype(jnp.bfloat16)
    d_query = (
        jnp.einsum(
            "kgst,tkd->skgd", scores_gradient, key_head_rows, preferred_element_type=jnp.float32
        )
        .astype(jnp.bfloat16)
        .reshape(sequence_length, heads_q * HEAD_SIZE)
    )
    key_gradient = (
        jnp.einsum(
            "apyq,yapz->qaz", scores_gradient, query_head_rows, preferred_element_type=jnp.float32
        )
        .astype(jnp.bfloat16)
        .reshape(sequence_length, heads_kv * HEAD_SIZE)
    )
    value_gradient = (
        jnp.einsum(
            "apyq,yapz->qaz",
            probability_batch,
            context_head_gradient,
            preferred_element_type=jnp.float32,
        )
        .astype(jnp.bfloat16)
        .reshape(sequence_length, heads_kv * HEAD_SIZE)
    )
    summed = jnp.einsum("sh,dh->sd", d_query, w_query, preferred_element_type=jnp.float32)
    summed = summed + jnp.einsum(
        "sh,dh->sd", key_gradient, w_key, preferred_element_type=jnp.float32
    )
    summed = summed + jnp.einsum(
        "sh,dh->sd", value_gradient, value_weight, preferred_element_type=jnp.float32
    )
    d_normed = lax.psum_scatter(
        convert_float(summed.astype(jnp.bfloat16)).astype(jnp.bfloat16),
        "tensor",
        scatter_dimension=0,
        tiled=True,
    ).astype(jnp.float32)
    gain_dn = d_normed * gain_vec
    grad_input = (
        convert_float(grad_local)
        + inv_rms * gain_dn
        - unit_rows * inv_rms * jnp.mean(gain_dn * unit_rows, axis=1, keepdims=True)
    ).astype(jnp.bfloat16)[None]
    gain_term = jnp.sum(d_normed * unit_rows, axis=0)
    query_term = convert_float(
        jnp.einsum("sd,sh->dh", full_normed, d_query, preferred_element_type=jnp.float32).astype(
            jnp.bfloat16
        )
    )
    key_term = convert_float(
        jnp.einsum(
            "sd,sh->dh", full_normed, key_gradient, preferred_element_type=jnp.float32
        ).astype(jnp.bfloat16)
    )
    value_term = convert_float(
        jnp.einsum(
            "sd,sh->dh", full_normed, value_gradient, preferred_element_type=jnp.float32
        ).astype(jnp.bfloat16)
    )
    sum_q, sum_k, sum_v, sum_o = (
        lax.psum_scatter(
            query_term.astype(jnp.bfloat16), "dp", scatter_dimension=0, tiled=True
        ).astype(jnp.float32),
        lax.psum_scatter(
            key_term.astype(jnp.bfloat16), "dp", scatter_dimension=0, tiled=True
        ).astype(jnp.float32),
        lax.psum_scatter(
            value_term.astype(jnp.bfloat16), "dp", scatter_dimension=0, tiled=True
        ).astype(jnp.float32),
        lax.psum_scatter(
            wout_term.astype(jnp.bfloat16), "dp", scatter_dimension=1, tiled=True
        ).astype(jnp.float32),
    )
    grad_wout = sum_o.astype(jnp.bfloat16)
    grad_gain = lax.psum(gain_term, ("dp", "tensor"))
    return (
        layer_output,
        grad_input,
        grad_gain,
        sum_q.astype(jnp.bfloat16),
        sum_k.astype(jnp.bfloat16),
        sum_v.astype(jnp.bfloat16),
        grad_wout,
    )


def solution(mesh):
    in_specs = (
        P("dp", "tensor", None),
        P(),
        P(None, "tensor"),
        P(None, "tensor"),
        P(None, "tensor"),
        P("tensor", None),
        P("dp"),
        P("dp", "tensor", None),
    )
    out_specs = (
        P("dp", "tensor", None),
        P("dp", "tensor", None),
        P(),
        P("dp", "tensor"),
        P("dp", "tensor"),
        P("dp", "tensor"),
        P("tensor", "dp"),
    )
    return jax.shard_map(
        per_device, mesh=mesh, in_specs=in_specs, out_specs=out_specs, check_vma=False
    )
```

profile of v0, /device:TPU:0, one launch (start us, length us, event | category | flops | bytes accessed | tf_op | source)
XLA Modules:
  0.0 1053.5 jit_solution(10929260345079268711)
XLA Ops:
  7.2 0.0 copy-start
  7.2 0.0 all-gather.4.cloned.1.call-start
  7.2 1.7 fusion.33
  8.9 0.7 convert_element_type.121
  9.6 2.5 fusion.29
  12.1 0.0 all-gather.4.cloned.1.call-update
  12.1 0.0 all-gather.6.cloned.1.call-start
  12.2 0.7 all-gather.6.cloned.1.call-update
  12.9 0.0 reduce-scatter.9.cloned.1.call-start
  13.6 0.3 fusion.19
  14.0 169.2 %all-gather.4.cloned.1.call-done = bf16[1024,4096]{1,0:T(8,128)(2,1)} async-done(((bf16[128,4096]{1,0:T(8,128)(2,1)}), bf16[1024,4096]{1,0:T(8,128)(2,1)}) %all-gather.4.cloned.1.call-update) | async-done | bytes 8388624 | tf_op jit(solution)/shard_map/all_gather | solution.py:28
  183.2 6.1 fusion.53
  189.3 0.0 copy-start.16
  189.3 2.4 convolution_convert_fusion.4
  191.7 0.0 copy-start.10
  191.7 0.8 copy-done.10
  192.5 1.9 fusion.10
  194.4 3.2 copy-done.2
  197.6 2.3 fusion.9
  199.9 156.0 %all-gather.6.cloned.1.call-done = bf16[1,1024,4096]{2,1,0:T(8,128)(2,1)} async-done(((bf16[1,128,4096]{2,1,0:T(8,128)(2,1)}), bf16[1,1024,4096]{2,1,0:T(8,128)(2,1)}) %all-gather.6.cloned.1.call-update) | async-done | bytes 8388624 | tf_op jit(solution)/shard_map/all_gather | solution.py:71
  355.9 6.5 fusion.35
  362.4 0.0 copy-start.8
  362.4 3.7 fusion.48
  366.2 2.3 fusion.52
  368.5 3.4 fusion
  371.9 0.0 copy-start.11
  371.9 0.0 copy-start.17
  371.9 3.6 fusion.14
  375.5 1.5 fusion.51
  377.1 0.7 convolution_convert_fusion.5
  377.8 0.0 copy-start.5
  377.8 0.0 copy-start.7
  377.8 8.1 fusion.58
  386.0 8.1 fusion.59
  394.1 15.3 %add_convert_fusion = bf16[1024,4096]{1,0:T(8,128)(2,1)} fusion(f32[1024,4096]{1,0:T(8,128)} %fusion.58, f32[1024,4096]{1,0:T(8,128)} %fusion.59, bf16[1024,128]{0,1:T(8,128)(2,1)S(1)} %copy-done.14, bf16[4096,128]{1,0:T(8,128)(2,1)S(1)} %copy-done.9), kind=kOutput, calls=%fused_computation | convolution fusion | flops 1086324736 | bytes 43253760 | tf_op jit(solution)/shard_map/sh,dh->sd/dot_general | solution.py:116
  409.4 0.0 reduce-scatter.9.cloned.1.call-update
  409.5 0.0 copy-start.6
  409.5 0.2 reduce-scatter.7.cloned.1.call-start
  409.7 6.4 fusion.38
  416.1 0.8 copy-done.12
  416.9 6.0 convolution_convert_fusion
  422.9 0.0 reduce-scatter.7.cloned.1.call-update
  422.9 0.0 reduce-scatter.15.cloned.1.call-start
  423.0 6.8 convolution_convert_fusion.2
  429.7 0.0 reduce-scatter.15.cloned.1.call-update
  429.8 0.0 reduce-scatter.13.cloned.1.call-start
  429.8 6.9 convolution_convert_fusion.3
  436.7 0.0 reduce-scatter.13.cloned.1.call-update
  436.7 0.0 reduce-scatter.17.cloned.1.call-start
  436.8 7.2 fusion.11
  443.9 0.0 reduce-scatter.17.cloned.1.call-update
  444.0 0.3 reduce-scatter.11.cloned.1.call-start
  444.2 0.0 copy-start.1
  444.3 7.4 convolution_convert_fusion.1
  451.7 0.0 reduce-scatter.11.cloned.1.call-update
  451.7 129.9 %reduce-scatter.9.cloned.1.call-done = bf16[128,4096]{1,0:T(8,128)(2,1)} async-done(((bf16[1024,4096]{1,0:T(8,128)(2,1)}), bf16[128,4096]{1,0:T(8,128)(2,1)}) %reduce-scatter.9.cloned.1.call-update) | async-done | bytes 1048592 | tf_op jit(solution)/shard_map/reduce_scatter | solution.py:119
  581.6 2.0 fusion.32
  583.6 100.6 %psum.7 = f32[4096]{0:T(1024)} all-reduce(f32[4096]{0:T(1024)S(1)} %get-tuple-element.7), channel_id=1, replica_groups=mesh['dp'=16,'tensor'=8] {'dp','tensor'}, use_global_device_ids=true, to_apply=%region_8.9 | all-reduce | flops 4096 | bytes 32768 | tf_op jit(solution)/shard_map/psum | solution.py:162
  684.2 71.1 %reduce-scatter.7.cloned.1.call-done = bf16[128,4096]{1,0:T(8,128)(2,1)} async-done(((bf16[1024,4096]{1,0:T(8,128)(2,1)}), bf16[128,4096]{1,0:T(8,128)(2,1)}) %reduce-scatter.7.cloned.1.call-update) | async-done | bytes 1048592 | tf_op jit(solution)/shard_map/reduce_scatter | solution.py:63
  755.3 4.2 fusion.55
  759.5 67.9 %reduce-scatter.15.cloned.1.call-done = bf16[256,128]{1,0:T(8,128)(2,1)} async-done(((bf16[4096,128]{1,0:T(8,128)(2,1)}), bf16[256,128]{1,0:T(8,128)(2,1)}) %reduce-scatter.15.cloned.1.call-update) | async-done | bytes 65552 | tf_op jit(solution)/shard_map/reduce_scatter | solution.py:154
  827.3 70.2 %reduce-scatter.13.cloned.1.call-done = bf16[256,128]{1,0:T(8,128)(2,1)} async-done(((bf16[4096,128]{1,0:T(8,128)(2,1)}), bf16[256,128]{1,0:T(8,128)(2,1)}) %reduce-scatter.13.cloned.1.call-update) | async-done | bytes 65552 | tf_op jit(solution)/shard_map/reduce_scatter | solution.py:151
  897.5 74.4 %reduce-scatter.17.cloned.1.call-done = bf16[256,256]{1,0:T(8,128)(2,1)} async-done(((bf16[256,4096]{1,0:T(8,128)(2,1)}), bf16[256,256]{1,0:T(8,128)(2,1)}) %reduce-scatter.17.cloned.1.call-update) | async-done | bytes 131088 | tf_op jit(solution)/shard_map/reduce_scatter | solution.py:157
  972.0 74.4 %reduce-scatter.11.cloned.1.call-done = bf16[256,256]{1,0:T(8,128)(2,1)} async-done(((bf16[4096,256]{1,0:T(8,128)(2,1)}), bf16[256,256]{1,0:T(8,128)(2,1)}) %reduce-scatter.11.cloned.1.call-update) | async-done | bytes 131088 | tf_op jit(solution)/shard_map/reduce_scatter | solution.py:148
  (35 shorter events, 0.1 us)
Async XLA Ops:
  7.2 182.1 %copy-start = (bf16[4096,256]{1,0:T(8,128)(2,1)S(1)}, bf16[4096,256]{1,0:T(8,128)(2,1)}, u32[]{:S(2)}) copy-start(bf16[4096,256]{1,0:T(8,128)(2,1)} %param.10) | copy-start | bytes 6291460
  7.2 176.0 %all-gather.4.cloned.1.call-start = ((), (), s32[]{:S(2)}) async-start(), calls=%async_computation.6 | async-start | bytes 9437184 | tf_op jit(solution)/shard_map/all_gather | solution.py:28
  12.1 343.8 %all-gather.6.cloned.1.call-start = ((), (), s32[]{:S(2)}) async-start(), calls=%async_computation.13 | async-start | bytes 9437184 | tf_op jit(solution)/shard_map/all_gather | solution.py:71
  12.9 568.7 %reduce-scatter.9.cloned.1.call-start = ((), (), s32[]{:S(2)}) async-start(), calls=%async_computation.8 | async-start | bytes 9437184 | tf_op jit(solution)/shard_map/reduce_scatter | solution.py:119
  183.2 6.1 copy-start.18
  189.3 2.4 copy-start.16
  191.7 0.8 copy-start.10
  194.4 3.2 copy-start.2
  355.9 6.5 copy-start.3
  355.9 10.2 slice-start
  362.4 3.7 copy-start.8
  362.4 3.7 slice-start.1
  368.5 3.4 copy-start.19
  371.9 3.6 copy-start.11
  371.9 5.2 copy-start.17
  377.8 8.2 copy-start.5
  377.8 8.2 copy-start.7
  386.0 8.1 copy-start.9
  386.0 8.1 copy-start.14
  409.5 7.4 copy-start.6
  409.5 345.8 %reduce-scatter.7.cloned.1.call-start = ((), (), s32[]{:S(2)}) async-start(), calls=%async_computation.7 | async-start | bytes 9437184 | tf_op jit(solution)/shard_map/reduce_scatter | solution.py:63
  416.1 0.8 copy-start.12
  416.9 6.1 copy-start.15
  422.9 404.4 %reduce-scatter.15.cloned.1.call-start = ((), (), s32[]{:S(2)}) async-start(), calls=%async_computation.11 | async-start | bytes 1114112 | tf_op jit(solution)/shard_map/reduce_scatter | solution.py:154
  429.7 7.0 copy-start.13
  429.8 467.8 %reduce-scatter.13.cloned.1.call-start = ((), (), s32[]{:S(2)}) async-start(), calls=%async_computation.10 | async-start | bytes 1114112 | tf_op jit(solution)/shard_map/reduce_scatter | solution.py:151
  436.7 535.3 %reduce-scatter.17.cloned.1.call-start = ((), (), s32[]{:S(2)}) async-start(), calls=%async_computation.12 | async-start | bytes 2228224 | tf_op jit(solution)/shard_map/reduce_scatter | solution.py:157
  444.0 137.6 %copy-start.4 = (bf16[1,128,4096]{2,1,0:T(8,128)(2,1)S(1)}, bf16[1,128,4096]{2,1,0:T(8,128)(2,1)}, u32[]{:S(2)}) copy-start(bf16[1,128,4096]{2,1,0:T(8,128)(2,1)} %param.8) | copy-start | bytes 3145732
  444.0 602.5 %reduce-scatter.11.cloned.1.call-start = ((), (), s32[]{:S(2)}) async-start(), calls=%async_computation.9 | async-start | bytes 2228224 | tf_op jit(solution)/shard_map/reduce_scatter | solution.py:148
  444.2 602.2 %copy-start.1 = (bf16[4096,256]{1,0:T(8,128)(2,1)S(1)}, bf16[4096,256]{1,0:T(8,128)(2,1)}, u32[]{:S(2)}) copy-start(bf16[4096,256]{1,0:T(8,128)(2,1)} %param.10) | copy-start | bytes 6291460
Sparse Core Ops, SparseCore 0:
  12.3 170.8 all-gather.3
  184.8 171.0 all-gather.5
  409.6 171.9 reduce-scatter.8
  583.8 171.4 reduce-scatter.6
  759.5 67.7 reduce-scatter.14
  831.6 65.9 reduce-scatter.12
  902.1 69.8 reduce-scatter.16
  976.5 69.8 reduce-scatter.10
where the time goes:
time: 1060 us; the launch traced here: 1050 us
  waiting for transfers between devices  814 us (77%)
  matrix products  101 us (10%)
  blocking collectives  101 us (10%)
  other arithmetic  17.3 us (2%)
  between operations  15.3 us (1%)
    all_gather x1, waiting for transfers between devices, per_device(): full_normed = lax.all_gather(normed, 'tensor', axis=0, tiled=True)  169 us
    all_gather x1, waiting for transfers between devices, per_device(): full_grad = lax.all_gather(grad_local, 'tensor', axis=0, tiled=True)  156 us
    reduce_scatter x1, waiting for transfers between devices, per_device(): lax.psum_scatter(convert_float(summed.astype(jnp.bfloat16)).astype(jnp.bf...  130 us
    psum x1, blocking collectives, per_device(): grad_gain = lax.psum(gain_term, ('dp', 'tensor'))  101 us
    reduce_scatter x1, waiting for transfers between devices, per_device(): lax.psum_scatter(query_term.astype(jnp.bfloat16), 'dp', scatter_dimension...  74.4 us
    reduce_scatter x1, waiting for transfers between devices, per_device(): lax.psum_scatter(wout_term.astype(jnp.bfloat16), 'dp', scatter_dimension=...  74.4 us
    reduce_scatter x1, waiting for transfers between devices, per_device(): lax.psum_scatter(convert_float(product.astype(jnp.bfloat16)).astype(jnp.b...  71.1 us
    reduce_scatter x1, waiting for transfers between devices, per_device(): lax.psum_scatter(key_term.astype(jnp.bfloat16), 'dp', scatter_dimension=0...  70.2 us
  transfers between devices with their start and end apart: 8, of which 8 were waited for; matrix products, arithmetic and copies ran while one was open for 6% of the time, Pallas kernels for 0%

commit v1 on v0

--- a/solution.py
+++ b/solution.py
@@ -8,9 +8,88 @@
 
 EPS = 1e-05
 
+NY = 4
+NZ = 2
+
 
 def convert_float(value):
     return value.astype(jnp.float32)
+
+
+def _t(y, z):
+    return (y % NY) * NZ + z
+
+
+def _perm(fn):
+    return [(t, fn(t)) for t in range(NY * NZ)]
+
+
+YP = _perm(lambda t: _t(t // NZ + 1, t % NZ))
+YM = _perm(lambda t: _t(t // NZ - 1, t % NZ))
+ZZ = _perm(lambda t: t ^ 1)
+
+SLOTS = ((0, 0), (-1, 0), (1, 0), (0, 1), (2, 0), (1, 1), (-1, 1), (2, 1))
+
+
+def _pp(x, perm):
+    return lax.ppermute(x, "tensor", perm)
+
+
+def _thirds(cols):
+    tiles = cols // 128
+    a = (tiles + 2) // 3
+    b = (tiles - a + 1) // 2
+    return [(0, a * 128), (a * 128, (a + b) * 128), ((a + b) * 128, cols)]
+
+
+def slot_tensor_index(me):
+    y = me // NZ
+    z = me % NZ
+    return [_t(y + dy, z ^ dz) for dy, dz in SLOTS]
+
+
+def gather_tensor(x):
+    rows, cols = x.shape
+    h = rows // 2
+    a = _pp(x, YP)
+    b = _pp(x, YM)
+    c = _pp(x, ZZ)
+    s_ym = _pp(jnp.concatenate([b[:h], c[:h]], 0), YM)
+    s_yp = _pp(jnp.concatenate([a[h:], c[h:]], 0), YP)
+    s_z = _pp(jnp.concatenate([b[h:], a[:h]], 0), ZZ)
+    d = jnp.concatenate([s_ym[:h], s_yp[:h]], 0)
+    e = jnp.concatenate([s_ym[h:], s_z[:h]], 0)
+    f = jnp.concatenate([s_z[h:], s_yp[h:]], 0)
+    (c0a, c0b), (c1a, c1b), (c2a, c2b) = _thirds(cols)
+    g0 = _pp(d[:, c0a:c0b], ZZ)
+    g1 = _pp(e[:, c1a:c1b], YM)
+    g2 = _pp(f[:, c2a:c2b], YP)
+    g = jnp.concatenate([g0, g1, g2], 1)
+    return jnp.concatenate([x, a, b, c, d, e, f, g], 0)
+
+
+def scatter_tensor(full, link_dtype):
+    rows = full.shape[0] // len(SLOTS)
+    cols = full.shape[1]
+    h = rows // 2
+    me, a, b, c, d, e, f, g = [full[i * rows:(i + 1) * rows] for i in range(len(SLOTS))]
+    (c0a, c0b), (c1a, c1b), (c2a, c2b) = _thirds(cols)
+    r_z = _pp(g[:, c0a:c0b].astype(link_dtype), ZZ)
+    r_yp = _pp(g[:, c1a:c1b].astype(link_dtype), YP)
+    r_ym = _pp(g[:, c2a:c2b].astype(link_dtype), YM)
+    d = jnp.concatenate([d[:, :c0b] + convert_float(r_z), d[:, c0b:]], 1)
+    e = jnp.concatenate([e[:, :c1a], e[:, c1a:c1b] + convert_float(r_yp), e[:, c1b:]], 1)
+    f = jnp.concatenate([f[:, :c2a], f[:, c2a:] + convert_float(r_ym)], 1)
+    s_yp = convert_float(_pp(jnp.concatenate([d[:h], e[:h]], 0).astype(link_dtype), YP))
+    s_ym = convert_float(_pp(jnp.concatenate([d[h:], f[h:]], 0).astype(link_dtype), YM))
+    s_z = convert_float(_pp(jnp.concatenate([e[h:], f[:h]], 0).astype(link_dtype), ZZ))
+    b = b + jnp.concatenate([s_yp[:h], s_z[:h]], 0)
+    c = c + jnp.concatenate([s_yp[h:], s_ym[h:]], 0)
+    a = a + jnp.concatenate([s_z[h:], s_ym[:h]], 0)
+    from_a = convert_float(_pp(a.astype(link_dtype), YM))
+    from_b = convert_float(_pp(b.astype(link_dtype), YP))
+    from_c = convert_float(_pp(c.astype(link_dtype), ZZ))
+    return me + from_a + from_b + from_c
 
 
 def per_device(
@@ -21,12 +100,22 @@
     heads_per_group = heads_q // heads_kv
     scale_f = 1.0 / HEAD_SIZE**0.5
     rows_f = convert_float(layer_input[0])
+    block_rows = rows_f.shape[0]
     gain_vec = convert_float(norm_gain)
     inv_rms = lax.rsqrt(jnp.mean(rows_f * rows_f, axis=1, keepdims=True) + EPS)
     unit_rows = rows_f * inv_rms
     normed = (unit_rows * gain_vec).astype(jnp.bfloat16)
-    full_normed = lax.all_gather(normed, "tensor", axis=0, tiled=True)
+    grad_local = grad_output[0]
+    full_normed = gather_tensor(normed)
+    full_grad = gather_tensor(grad_local)
     sequence_length = full_normed.shape[0]
+
+    me = lax.axis_index("tensor")
+    slot_t = jnp.stack(slot_tensor_index(me)).astype(jnp.int32)
+    positions = (
+        slot_t[:, None] * block_rows + lax.iota(jnp.int32, block_rows)[None, :]
+    ).reshape(sequence_length)
+
     query_matrix = jnp.dot(full_normed, w_query, preferred_element_type=jnp.float32).astype(
         jnp.bfloat16
     )
@@ -39,7 +128,6 @@
     query_head_rows = query_matrix.reshape(sequence_length, heads_kv, heads_per_group, HEAD_SIZE)
     key_head_rows = key_projected.reshape(sequence_length, heads_kv, HEAD_SIZE)
     value_head_rows = value_projected.reshape(sequence_length, heads_kv, HEAD_SIZE)
-    positions = lax.iota(jnp.int32, sequence_length)
     allowed = (positions[None, :] <= positions[:, None]) | (positions[None, :] < prefix_len[0])
     scores = (
         jnp.einsum(
@@ -60,23 +148,14 @@
         .reshape(sequence_length, heads_q * HEAD_SIZE)
     )
     product = jnp.dot(context, w_out, preferred_element_type=jnp.float32)
-    attn_sum = lax.psum_scatter(
-        convert_float(product.astype(jnp.bfloat16)).astype(jnp.bfloat16),
-        "tensor",
-        scatter_dimension=0,
-        tiled=True,
-    ).astype(jnp.float32)
+    attn_sum = scatter_tensor(convert_float(product.astype(jnp.bfloat16)), jnp.bfloat16)
     layer_output = (rows_f + attn_sum).astype(jnp.bfloat16)[None]
-    grad_local = grad_output[0]
-    full_grad = lax.all_gather(grad_local, "tensor", axis=0, tiled=True)
     context_gradient = jnp.einsum(
         "sd,hd->sh", full_grad, w_out, preferred_element_type=jnp.float32
     ).astype(jnp.bfloat16)
-    wout_term = convert_float(
-        jnp.einsum("sh,sd->hd", context, full_grad, preferred_element_type=jnp.float32).astype(
-            jnp.bfloat16
-        )
-    )
+    wout_term = jnp.einsum(
+        "sh,sd->hd", context, full_grad, preferred_element_type=jnp.float32
+    ).astype(jnp.bfloat16)
     context_head_gradient = context_gradient.reshape(
         sequence_length, heads_kv, heads_per_group, HEAD_SIZE
     )
@@ -116,12 +195,7 @@
     summed = summed + jnp.einsum(
         "sh,dh->sd", value_gradient, value_weight, preferred_element_type=jnp.float32
     )
-    d_normed = lax.psum_scatter(
-        convert_float(summed.astype(jnp.bfloat16)).astype(jnp.bfloat16),
-        "tensor",
-        scatter_dimension=0,
-        tiled=True,
-    ).astype(jnp.float32)
+    d_normed = scatter_tensor(convert_float(summed.astype(jnp.bfloat16)), jnp.bfloat16)
     gain_dn = d_normed * gain_vec
     grad_input = (
         convert_float(grad_local)
@@ -129,44 +203,45 @@
         - unit_rows * inv_rms * jnp.mean(gain_dn * unit_rows, axis=1, keepdims=True)
     ).astype(jnp.bfloat16)[None]
     gain_term = jnp.sum(d_normed * unit_rows, axis=0)
-    query_term = convert_float(
-        jnp.einsum("sd,sh->dh", full_normed, d_query, preferred_element_type=jnp.float32).astype(
-            jnp.bfloat16
-        )
-    )
-    key_term = convert_float(
-        jnp.einsum(
-            "sd,sh->dh", full_normed, key_gradient, preferred_element_type=jnp.float32
-        ).astype(jnp.bfloat16)
-    )
-    value_term = convert_float(
-        jnp.einsum(
-            "sd,sh->dh", full_normed, value_gradient, preferred_element_type=jnp.float32
-        ).astype(jnp.bfloat16)
-    )
-    sum_q, sum_k, sum_v, sum_o = (
-        lax.psum_scatter(
-            query_term.astype(jnp.bfloat16), "dp", scatter_dimension=0, tiled=True
-        ).astype(jnp.float32),
-        lax.psum_scatter(
-            key_term.astype(jnp.bfloat16), "dp", scatter_dimension=0, tiled=True
-        ).astype(jnp.float32),
-        lax.psum_scatter(
-            value_term.astype(jnp.bfloat16), "dp", scatter_dimension=0, tiled=True
-        ).astype(jnp.float32),
-        lax.psum_scatter(
-            wout_term.astype(jnp.bfloat16), "dp", scatter_dimension=1, tiled=True
-        ).astype(jnp.float32),
-    )
-    grad_wout = sum_o.astype(jnp.bfloat16)
+    query_term = jnp.einsum(
+        "sd,sh->dh", full_normed, d_query, preferred_element_type=jnp.float32
+    ).astype(jnp.bfloat16)
+    key_term = jnp.einsum(
+        "sd,sh->dh", full_normed, key_gradient, preferred_element_type=jnp.float32
+    ).astype(jnp.bfloat16)
+    value_term = jnp.einsum(
+        "sd,sh->dh", full_normed, value_gradient, preferred_element_type=jnp.float32
+    ).astype(jnp.bfloat16)
+    n_dp = lax.psum(1, "dp")
+    width = query_term.shape[0]
+    out_rows = w_out.shape[0]
+    wq_cols = query_term.shape[1]
+    wk_cols = key_term.shape[1]
+    wv_cols = value_term.shape[1]
+    wo_cols = width // n_dp
+    wout_blocks = wout_term.reshape(out_rows, n_dp, wo_cols).transpose(1, 0, 2)
+    packed = jnp.concatenate(
+        [
+            query_term.reshape(n_dp, width // n_dp, wq_cols),
+            key_term.reshape(n_dp, width // n_dp, wk_cols),
+            value_term.reshape(n_dp, width // n_dp, wv_cols),
+            wout_blocks,
+        ],
+        axis=2,
+    )
+    reduced = lax.psum_scatter(packed, "dp", scatter_dimension=0, tiled=True)[0]
+    sum_q = reduced[:, :wq_cols]
+    sum_k = reduced[:, wq_cols:wq_cols + wk_cols]
+    sum_v = reduced[:, wq_cols + wk_cols:wq_cols + wk_cols + wv_cols]
+    grad_wout = reduced[:, wq_cols + wk_cols + wv_cols:]
     grad_gain = lax.psum(gain_term, ("dp", "tensor"))
     return (
         layer_output,
         grad_input,
         grad_gain,
-        sum_q.astype(jnp.bfloat16),
-        sum_k.astype(jnp.bfloat16),
-        sum_v.astype(jnp.bfloat16),
+        sum_q,
+        sum_k,
+        sum_v,
         grad_wout,
     )
 

time: 1060 us -> 462 us (0.44)
  waiting for transfers between devices: 814 us -> 132 us
  starting transfers between devices: 0.71 us -> 54 us
  local copies, waits for them, and re-layouts: 4.88 us -> 36.1 us
  blocking collectives: 101 us -> 72.5 us
  other arithmetic: 17.3 us -> 45 us
    reduce_scatter x6 -> x1, waiting for transfers between devices: 488 us -> 0.01 us  [per_device(): reduced = lax.psum_scatter(packed, 'dp', scatter_dimension=0, tiled=True)[0]]
    all_gather x2 -> x0, waiting for transfers between devices: 325 us -> none  [the longest x1 169 us: per_device(): full_normed = lax.all_gather(normed, 'tensor', axis=0, tiled=True)]
    ppermute x0 -> x36, waiting for transfers between devices: none -> 132 us  [_pp(): return lax.ppermute(x, 'tensor', perm)]
    ppermute x0 -> x36, starting transfers between devices: none -> 54 us  [_pp(): return lax.ppermute(x, 'tensor', perm)]
    psum x1, blocking collectives: 101 us -> 72.5 us  [per_device(): grad_gain = lax.psum(gain_term, ('dp', 'tensor'))]
    slice x0 -> x34, local copies, waits for them, and re-layouts: none -> 21.6 us  [the longest x2 3.53 us: scatter_tensor(): e[:, :c1a]]
  transfers between devices with their start and end apart: 8 -> 37, of which waited for: 8 -> 17; matrix products, arithmetic and copies ran while one was open for 6% -> 13% of each run, Pallas kernels for 0% -> 0%
where the time goes in v1:
time: 462 us; the launch traced here: 453 us
  waiting for transfers between devices  132 us (29%)
  matrix products  96.5 us (21%)
  blocking collectives  72.5 us (16%)
  starting transfers between devices  54 us (12%)
  other arithmetic  45 us (10%)
  local copies, waits for them, and re-layouts  36.1 us (8%)
  between operations  16.3 us (4%)
    ppermute x36, waiting for transfers between devices, _pp(): return lax.ppermute(x, 'tensor', perm)  132 us
    psum x1, blocking collectives, per_device(): grad_gain = lax.psum(gain_term, ('dp', 'tensor'))  72.5 us
    ppermute x36, starting transfers between devices, _pp(): return lax.ppermute(x, 'tensor', perm)  54 us
    dot_general x1, matrix products, per_device(): jnp.einsum('sh,dh->sd', value_gradient, value_weight, preferred_element_t...  21.1 us
    unnamed x81, local copies, waits for them, and re-layouts  14.2 us
    another operation x5, other arithmetic  12.5 us
  transfers between devices with their start and end apart: 37, of which 17 were waited for; matrix products, arithmetic and copies ran while one was open for 13% of the time, Pallas kernels for 0%

profile of v1, /device:TPU:0, one launch (start us, length us, event | category | flops | bytes accessed | tf_op | source)
XLA Modules:
  0.0 452.9 jit_solution(14844425756664865842)
XLA Ops:
  7.2 3.2 collective-permute-start.19
  10.4 1.9 collective-permute-start.20
  15.2 3.0 constant_dynamic-update-slice_fusion.8
  18.3 3.2 collective-permute-start.1
  24.7 9.6 %collective-permute-done.19 = bf16[128,4096]{1,0:T(8,128)(2,1)S(1)} collective-permute-done((bf16[128,4096]{1,0:T(8,128)(2,1)}, bf16[128,4096]{1,0:T(8,128)(2,1)S(1)}, u32[]{:S(2)}, u32[]{:S(2)}) %collective-permute-start.19) | collective-permute-done | bytes 1048608 | tf_op jit(solution)/shard_map/ppermute | solution.py:35
  37.9 2.0 collective-permute-start.23
  42.9 16.4 %collective-permute-done.2 = bf16[128,4096]{1,0:T(8,128)(2,1)} collective-permute-done((bf16[128,4096]{1,0:T(8,128)(2,1)}, bf16[128,4096]{1,0:T(8,128)(2,1)}, u32[]{:S(2)}, u32[]{:S(2)}) %collective-permute-start.2) | collective-permute-done | bytes 1048608 | tf_op jit(solution)/shard_map/ppermute | solution.py:35
  62.6 2.7 collective-permute-start.3
  71.3 7.8 %collective-permute-done.21 = bf16[128,4096]{1,0:T(8,128)(2,1)S(1)} collective-permute-done((bf16[128,4096]{1,0:T(8,128)(2,1)S(1)}, bf16[128,4096]{1,0:T(8,128)(2,1)S(1)}, u32[]{:S(2)}, u32[]{:S(2)}) %collective-permute-start.21) | collective-permute-done | bytes 1048608 | tf_op jit(solution)/shard_map/ppermute | solution.py:35
  79.1 1.9 collective-permute-start.5
  81.3 3.8 collective-permute-start.25
  86.7 14.9 %collective-permute-done.3 = bf16[128,4096]{1,0:T(8,128)(2,1)S(1)} collective-permute-done((bf16[128,4096]{1,0:T(8,128)(2,1)S(1)}, bf16[128,4096]{1,0:T(8,128)(2,1)S(1)}, u32[]{:S(2)}, u32[]{:S(2)}) %collective-permute-start.3) | collective-permute-done | bytes 1048608 | tf_op jit(solution)/shard_map/ppermute | solution.py:35
  101.7 7.2 %collective-permute-done.4 = bf16[128,4096]{1,0:T(8,128)(2,1)S(1)} collective-permute-done((bf16[128,4096]{1,0:T(8,128)(2,1)S(1)}, bf16[128,4096]{1,0:T(8,128)(2,1)S(1)}, u32[]{:S(2)}, u32[]{:S(2)}) %collective-permute-start.4) | collective-permute-done | bytes 1048608 | tf_op jit(solution)/shard_map/ppermute | solution.py:35
  109.1 2.0 collective-permute-start.6
  111.4 3.3 collective-permute-start.7
  115.0 4.8 %collective-permute-done.8 = bf16[128,1280]{1,0:T(8,128)(2,1)S(1)} collective-permute-done((bf16[128,1280]{1,0:T(8,128)(2,1)S(1)}, bf16[128,1280]{1,0:T(8,128)(2,1)S(1)}, u32[]{:S(2)}, u32[]{:S(2)}) %collective-permute-start.8) | collective-permute-done | bytes 327712 | tf_op jit(solution)/shard_map/ppermute | solution.py:35
  119.8 1.7 collective-permute-start.24
  121.6 3.2 copy-done.20
  124.9 2.3 fusion.50
  127.2 5.9 %convolution_convert_fusion.6 = bf16[1024,256]{0,1:T(8,128)(2,1)S(1)} fusion(bf16[1024,4096]{1,0:T(8,128)(2,1)} %copy-done.20, bf16[4096,256]{1,0:T(8,128)(2,1)S(1)} %copy-done.6), kind=kOutput, calls=%fused_computation.66 | convolution fusion | flops 2147745792 | bytes 11010048 | tf_op jit(solution)/shard_map/dot_general | solution.py:119
  133.1 5.9 %fusion.49 = bf16[1024,128,1]{1,0,2:T(8,128)(2,1)S(1)} fusion(bf16[1024,4096]{1,0:T(8,128)(2,1)} %copy-done.20, bf16[4096,128]{1,0:T(8,128)(2,1)S(1)} %copy-done.10), kind=kOutput, calls=%fused_computation.77 | convolution fusion | flops 1073872896 | bytes 9699328 | tf_op jit(solution)/shard_map/dot_general | solution.py:125
  139.2 2.4 convolution_convert_fusion.5
  141.5 1.9 fusion.6
  143.4 2.0 fusion.5
  145.4 3.0 fusion.45
  148.4 3.8 fusion.35
  152.2 3.4 fusion
  155.6 11.8 %fusion.7 = bf16[2,1024,1024]{1,2,0:T(8,128)(2,1)S(1)} fusion(f32[1024,1024,2]{1,0,2:T(8,128)S(1)} %get-tuple-element.93, f32[2,1024]{1,0:T(2,128)S(1)} %get-tuple-element.92, f32[2,1024]{1,0:T(2,128)S(1)} %fusion.5, f32[2,1024]{1,0:T(2,128)S(1)} %get-tuple-element.90, f32[1024,1024,2]{1,0,2:T(8,128)S(1)} %get-tuple-element.91, ...), kind=kLoop, calls=%fused_computation.18 | loop fusion | flops 16777216 | bytes 22044672 | tf_op jit(solution)/shard_map/reshape.25
  169.7 7.3 %convolution_convert_fusion.2 = bf16[4096,256]{1,0:T(8,128)(2,1)} fusion(bf16[1024,4096]{1,0:T(8,128)(2,1)} %copy-done.20, bf16[1024,256]{0,1:T(8,128)(2,1)S(1)} %bitcast.172), kind=kOutput, calls=%fused_computation.15 | convolution fusion | flops 2148532224 | bytes 11010048 | tf_op jit(solution)/shard_map/sd,sh->dh/dot_general | solution.py:206
  177.0 8.2 %fusion.89 = f32[1024,4096]{1,0:T(8,128)} fusion(bf16[1024,256]{0,1:T(8,128)(2,1)S(1)} %bitcast.173, bf16[4096,256]{1,0:T(8,128)(2,1)S(1)} %copy-done.6), kind=kOutput, calls=%fused_computation.162 | convolution fusion | flops 2147483648 | bytes 19398656 | tf_op jit(solution)/shard_map/sh,dh->sd/dot_general | solution.py:191
  185.3 3.5 convolution_convert_fusion.4
  188.8 8.2 %fusion.90 = f32[1024,4096]{1,0:T(8,128)} fusion(bf16[1024,128]{0,1:T(8,128)(2,1)S(1)} %fusion.48, bf16[4096,128]{1,0:T(8,128)(2,1)S(1)} %copy-done.12), kind=kOutput, calls=%fused_computation.163 | convolution fusion | flops 1073741824 | bytes 18087936 | tf_op jit(solution)/shard_map/sh,dh->sd/dot_general | solution.py:192
  196.9 3.7 convolution_convert_fusion.3
  200.6 21.1 %fusion.87 = (f32[1024,4096]{1,0:T(8,128)}, bf16[1024,4096]{1,0:T(8,128)(2,1)}) fusion(bf16[1024,128]{0,1:T(8,128)(2,1)S(1)} %fusion.45, bf16[4096,128]{1,0:T(8,128)(2,1)S(1)} %copy-done.10, f32[1024,4096]{1,0:T(8,128)} %fusion.89, f32[1024,4096]{1,0:T(8,128)} %fusion.90), kind=kOutput, calls=%fused_computation.160 | convolution fusion | flops 1090519040 | bytes 60030976 | tf_op jit(solution)/shard_map/sh,dh->sd/dot_general | solution.py:195
  221.7 2.0 fusion.58
  223.7 2.0 slice.456
  226.9 2.2 fusion.57
  229.2 5.7 %convolution_convert_fusion.1 = bf16[256,4096]{1,0:T(8,128)(2,1)S(1)} fusion(bf16[1024,256]{0,1:T(8,128)(2,1)S(1)} %bitcast.181, bf16[1024,4096]{1,0:T(8,128)(2,1)} %copy-done.23), kind=kOutput, calls=%fused_computation.14 | convolution fusion | flops 2148532224 | bytes 11010048 | tf_op jit(solution)/shard_map/sh,sd->hd/dot_general | solution.py:156
  234.9 8.2 %fusion.88 = (f32[1024,4096]{1,0:T(8,128)}, bf16[1024,4096]{1,0:T(8,128)(2,1)S(1)}) fusion(bf16[1024,256]{0,1:T(8,128)(2,1)S(1)} %bitcast.182, bf16[256,4096]{1,0:T(8,128)(2,1)S(1)} %copy-done), kind=kOutput, calls=%fused_computation.161 | convolution fusion | flops 2155872256 | bytes 27787264 | tf_op jit(solution)/shard_map/dot_general | solution.py:150
  244.8 2.9 copy-done.2
  248.3 3.2 pad_maximum_fusion
  251.5 1.9 collective-permute-start.28
  254.2 2.6 collective-permute-start.10
  258.1 1.9 collective-permute-start.12
  262.5 2.1 collective-permute-done.10
  266.0 1.6 slice_add_fusion.9
  268.1 2.2 collective-permute-start.31
  271.9 2.1 slice_add_fusion.11
  274.5 3.3 collective-permute-start.13
  278.1 16.2 %collective-permute-done.31 = bf16[128,4096]{1,0:T(8,128)(2,1)S(1)} collective-permute-done((bf16[128,4096]{1,0:T(8,128)(2,1)S(1)}, bf16[128,4096]{1,0:T(8,128)(2,1)S(1)}, u32[]{:S(2)}, u32[]{:S(2)}) %collective-permute-start.31) | collective-permute-done | bytes 1048608 | tf_op jit(solution)/shard_map/ppermute | solution.py:35
  295.4 2.5 collective-permute-done.33
  298.2 3.4 collective-permute-done.29
  302.7 3.0 collective-permute-start.32
  305.8 2.5 collective-permute-start.35
  308.3 8.5 %collective-permute-done.13 = bf16[128,4096]{1,0:T(8,128)(2,1)S(1)} collective-permute-done((bf16[128,4096]{1,0:T(8,128)(2,1)S(1)}, bf16[128,4096]{1,0:T(8,128)(2,1)S(1)}, u32[]{:S(2)}, u32[]{:S(2)}) %collective-permute-start.13) | collective-permute-done | bytes 1048608 | tf_op jit(solution)/shard_map/ppermute | solution.py:35
  316.9 2.9 collective-permute-done.15
  320.1 14.8 %collective-permute-done.11 = bf16[128,4096]{1,0:T(8,128)(2,1)S(1)} collective-permute-done((bf16[128,4096]{1,0:T(8,128)(2,1)S(1)}, bf16[128,4096]{1,0:T(8,128)(2,1)S(1)}, u32[]{:S(2)}, u32[]{:S(2)}) %collective-permute-start.11) | collective-permute-done | bytes 1048608 | tf_op jit(solution)/shard_map/ppermute | solution.py:35
  335.1 4.4 fusion.32
  339.5 2.7 collective-permute-start.14
  343.8 17.7 %collective-permute-done.35 = bf16[128,4096]{1,0:T(8,128)(2,1)S(1)} collective-permute-done((bf16[128,4096]{1,0:T(8,128)(2,1)S(1)}, bf16[128,4096]{1,0:T(8,128)(2,1)S(1)}, u32[]{:S(2)}, u32[]{:S(2)}) %collective-permute-start.35) | collective-permute-done | bytes 1048608 | tf_op jit(solution)/shard_map/ppermute | solution.py:35
  361.6 2.1 fusion.22
  363.7 72.5 %psum.7 = f32[4096]{0:T(1024)} all-reduce(f32[4096]{0:T(1024)S(1)} %get-tuple-element.7), channel_id=1, replica_groups=mesh['dp'=16,'tensor'=8] {'dp','tensor'}, use_global_device_ids=true, to_apply=%region_6.7 | all-reduce | flops 4096 | bytes 32768 | tf_op jit(solution)/shard_map/psum | solution.py:237
  436.3 6.1 %fusion.52 = (bf16[1,128,4096]{2,1,0:T(8,128)(2,1)}, bf16[1,128,4096]{2,1,0:T(8,128)(2,1)}) fusion(f32[128,4096]{1,0:T(8,128)} %get-tuple-element.9, bf16[1,128,4096]{2,1,0:T(8,128)(2,1)S(1)} %copy-done.1, f32[128]{0:T(128)S(1)} %broadcast_multiply_fusion.1, f32[4096]{0:T(1024)S(1)} %copy-done.17, f32[128]{0:T(128)S(1)} %copy-done.25, ...), kind=kLoop, calls=%fused_computation.80 | loop fusion | flops 9437184 | bytes 11551744 | tf_op jit(solution)/shard_map/broadcast_in_dim | solution.py:200
  443.9 1.7 fusion.85
  (194 shorter events, 44.9 us)
Async XLA Ops:
  7.2 132.0 %copy-start = (bf16[256,4096]{1,0:T(8,128)(2,1)S(1)}, bf16[256,4096]{1,0:T(8,128)(2,1)}, u32[]{:S(2)}) copy-start(bf16[256,4096]{1,0:T(8,128)(2,1)} %param.13) | copy-start | bytes 6291460
  7.2 435.2 %reduce-scatter.2.cloned.1.call-start = ((), (), s32[]{:S(2)}) async-start(), calls=%async_computation.1 | async-start | bytes 6684672 | tf_op jit(solution)/shard_map/reduce_scatter | solution.py:232
  7.2 27.1 %collective-permute-start.19 = (bf16[128,4096]{1,0:T(8,128)(2,1)}, bf16[128,4096]{1,0:T(8,128)(2,1)S(1)}, u32[]{:S(2)}, u32[]{:S(2)}) collective-permute-start(bf16[128,4096]{1,0:T(8,128)(2,1)} %bitcast.174), channel_id=1, source_target_pairs={{0,6},{1,7},{2,0},{3,1},{4,2},{5,3},{6,4},{7,5},{8,14},{9,15},{10,... | collective-permute-start | bytes 3145736 | tf_op jit(solution)/shard_map/ppermute | solution.py:35
  10.4 26.1 %collective-permute-start.18 = (bf16[128,4096]{1,0:T(8,128)(2,1)}, bf16[128,4096]{1,0:T(8,128)(2,1)}, u32[]{:S(2)}, u32[]{:S(2)}) collective-permute-start(bf16[128,4096]{1,0:T(8,128)(2,1)} %bitcast.175), channel_id=1, source_target_pairs={{0,2},{1,3},{2,4},{3,5},{4,6},{5,7},{6,0},{7,1},{8,10},{9,11},{10,... | collective-permute-start | bytes 3145736 | tf_op jit(solution)/shard_map/ppermute | solution.py:35
  10.4 29.5 %collective-permute-start.20 = (bf16[128,4096]{1,0:T(8,128)(2,1)}, bf16[128,4096]{1,0:T(8,128)(2,1)}, u32[]{:S(2)}, u32[]{:S(2)}) collective-permute-start(bf16[128,4096]{1,0:T(8,128)(2,1)} %bitcast.176), channel_id=1, source_target_pairs={{0,1},{1,0},{2,3},{3,2},{4,5},{5,4},{6,7},{7,6},{8,9},{9,8},{10,11... | collective-permute-start | bytes 3145736 | tf_op jit(solution)/shard_map/ppermute | solution.py:35
  18.1 41.1 %collective-permute-start.2 = (bf16[128,4096]{1,0:T(8,128)(2,1)}, bf16[128,4096]{1,0:T(8,128)(2,1)}, u32[]{:S(2)}, u32[]{:S(2)}) collective-permute-start(bf16[128,4096]{1,0:T(8,128)(2,1)} %get-tuple-element.11), channel_id=1, source_target_pairs={{0,1},{1,0},{2,3},{3,2},{4,5},{5,4},{6,7},{7,6},{8,9},{9,8},{10,11... | collective-permute-start | bytes 3145736 | tf_op jit(solution)/shard_map/ppermute | solution.py:35
  18.3 42.8 %collective-permute-start.1 = (bf16[128,4096]{1,0:T(8,128)(2,1)}, bf16[128,4096]{1,0:T(8,128)(2,1)}, u32[]{:S(2)}, u32[]{:S(2)}) collective-permute-start(bf16[128,4096]{1,0:T(8,128)(2,1)} %get-tuple-element.11), channel_id=1, source_target_pairs={{0,6},{1,7},{2,0},{3,1},{4,2},{5,3},{6,4},{7,5},{8,14},{9,15},{10,... | collective-permute-start | bytes 3145736 | tf_op jit(solution)/shard_map/ppermute | solution.py:35
  34.3 31.1 %collective-permute-start = (bf16[128,4096]{1,0:T(8,128)(2,1)}, bf16[128,4096]{1,0:T(8,128)(2,1)S(1)}, u32[]{:S(2)}, u32[]{:S(2)}) collective-permute-start(bf16[128,4096]{1,0:T(8,128)(2,1)} %get-tuple-element.11), channel_id=1, source_target_pairs={{0,2},{1,3},{2,4},{3,5},{4,6},{5,7},{6,0},{7,1},{8,10},{9,11},{10,... | collective-permute-start | bytes 3145736 | tf_op jit(solution)/shard_map/ppermute | solution.py:35
  37.9 43.3 %collective-permute-start.23 = (bf16[128,4096]{1,0:T(8,128)(2,1)S(1)}, bf16[128,4096]{1,0:T(8,128)(2,1)S(1)}, u32[]{:S(2)}, u32[]{:S(2)}) collective-permute-start(bf16[128,4096]{1,0:T(8,128)(2,1)S(1)} %pad_maximum_fusion.9), channel_id=1, source_target_pairs={{0,1},{1,0},{2,3},{3,2},{4,5},{5,4},{6,7},{7,6},{8,9},{9,8},{10,11... | collective-permute-start | bytes 3145736 | tf_op jit(solution)/shard_map/ppermute | solution.py:35
  41.3 37.8 %collective-permute-start.21 = (bf16[128,4096]{1,0:T(8,128)(2,1)S(1)}, bf16[128,4096]{1,0:T(8,128)(2,1)S(1)}, u32[]{:S(2)}, u32[]{:S(2)}) collective-permute-start(bf16[128,4096]{1,0:T(8,128)(2,1)S(1)} %pad_maximum_fusion.7), channel_id=1, source_target_pairs={{0,6},{1,7},{2,0},{3,1},{4,2},{5,3},{6,4},{7,5},{8,14},{9,15},{10,... | collective-permute-start | bytes 3145736 | tf_op jit(solution)/shard_map/ppermute | solution.py:35
  59.2 27.2 %collective-permute-start.22 = (bf16[128,4096]{1,0:T(8,128)(2,1)S(1)}, bf16[128,4096]{1,0:T(8,128)(2,1)S(1)}, u32[]{:S(2)}, u32[]{:S(2)}) collective-permute-start(bf16[128,4096]{1,0:T(8,128)(2,1)S(1)} %pad_maximum_fusion.8), channel_id=1, source_target_pairs={{0,2},{1,3},{2,4},{3,5},{4,6},{5,7},{6,0},{7,1},{8,10},{9,11},{10,... | collective-permute-start | bytes 3145736 | tf_op jit(solution)/shard_map/ppermute | solution.py:35
  61.1 7.5 %slice-start.4 = ((s8[8388608]{0:T(1024)(128)(4,1)}), s8[4194304]{0:T(1024)(128)(4,1)S(1)}, s32[]{:S(2)}) async-start(s8[8388608]{0:T(1024)(128)(4,1)} %bitcast.187), calls=%async_computation.6 | async-start | bytes 8388608
  62.6 38.9 %collective-permute-start.3 = (bf16[128,4096]{1,0:T(8,128)(2,1)S(1)}, bf16[128,4096]{1,0:T(8,128)(2,1)S(1)}, u32[]{:S(2)}, u32[]{:S(2)}) collective-permute-start(bf16[128,4096]{1,0:T(8,128)(2,1)S(1)} %pad_maximum_fusion.1), channel_id=1, source_target_pairs={{0,6},{1,7},{2,0},{3,1},{4,2},{5,3},{6,4},{7,5},{8,14},{9,15},{10,... | collective-permute-start | bytes 3145736 | tf_op jit(solution)/shard_map/ppermute | solution.py:35
  65.6 43.4 %collective-permute-start.4 = (bf16[128,4096]{1,0:T(8,128)(2,1)S(1)}, bf16[128,4096]{1,0:T(8,128)(2,1)S(1)}, u32[]{:S(2)}, u32[]{:S(2)}) collective-permute-start(bf16[128,4096]{1,0:T(8,128)(2,1)S(1)} %pad_maximum_fusion.2), channel_id=1, source_target_pairs={{0,2},{1,3},{2,4},{3,5},{4,6},{5,7},{6,0},{7,1},{8,10},{9,11},{10,... | collective-permute-start | bytes 3145736 | tf_op jit(solution)/shard_map/ppermute | solution.py:35
  79.1 32.0 %collective-permute-start.5 = (bf16[128,4096]{1,0:T(8,128)(2,1)S(1)}, bf16[128,4096]{1,0:T(8,128)(2,1)S(1)}, u32[]{:S(2)}, u32[]{:S(2)}) collective-permute-start(bf16[128,4096]{1,0:T(8,128)(2,1)S(1)} %pad_maximum_fusion.3), channel_id=1, source_target_pairs={{0,1},{1,0},{2,3},{3,2},{4,5},{5,4},{6,7},{7,6},{8,9},{9,8},{10,11... | collective-permute-start | bytes 3145736 | tf_op jit(solution)/shard_map/ppermute | solution.py:35
  81.3 57.7 %collective-permute-start.25 = (bf16[128,1408]{1,0:T(8,128)(2,1)S(1)}, bf16[128,1408]{1,0:T(8,128)(2,1)S(1)}, u32[]{:S(2)}, u32[]{:S(2)}) collective-permute-start(bf16[128,1408]{1,0:T(8,128)(2,1)S(1)} %pad_maximum_fusion.13), channel_id=1, source_target_pairs={{0,6},{1,7},{2,0},{3,1},{4,2},{5,3},{6,4},{7,5},{8,14},{9,15},{10,... | collective-permute-start | bytes 1081352 | tf_op jit(solution)/shard_map/ppermute | solution.py:35
  86.6 52.4 %collective-permute-start.26 = (bf16[128,1280]{1,0:T(8,128)(2,1)S(1)}, bf16[128,1280]{1,0:T(8,128)(2,1)S(1)}, u32[]{:S(2)}, u32[]{:S(2)}) collective-permute-start(bf16[128,1280]{1,0:T(8,128)(2,1)S(1)} %pad_maximum_fusion.17), channel_id=1, source_target_pairs={{0,2},{1,3},{2,4},{3,5},{4,6},{5,7},{6,0},{7,1},{8,10},{9,11},{10,... | collective-permute-start | bytes 983048 | tf_op jit(solution)/shard_map/ppermute | solution.py:35
  109.1 12.4 %collective-permute-start.6 = (bf16[128,1408]{1,0:T(8,128)(2,1)S(1)}, bf16[128,1408]{1,0:T(8,128)(2,1)S(1)}, u32[]{:S(2)}, u32[]{:S(2)}) collective-permute-start(bf16[128,1408]{1,0:T(8,128)(2,1)S(1)} %pad_maximum_fusion.16), channel_id=1, source_target_pairs={{0,1},{1,0},{2,3},{3,2},{4,5},{5,4},{6,7},{7,6},{8,9},{9,8},{10,11... | collective-permute-start | bytes 1081352 | tf_op jit(solution)/shard_map/ppermute | solution.py:35
  111.2 8.6 %collective-permute-start.8 = (bf16[128,1280]{1,0:T(8,128)(2,1)S(1)}, bf16[128,1280]{1,0:T(8,128)(2,1)S(1)}, u32[]{:S(2)}, u32[]{:S(2)}) collective-permute-start(bf16[128,1280]{1,0:T(8,128)(2,1)S(1)} %pad_maximum_fusion.18), channel_id=1, source_target_pairs={{0,2},{1,3},{2,4},{3,5},{4,6},{5,7},{6,0},{7,1},{8,10},{9,11},{10,... | collective-permute-start | bytes 983048 | tf_op jit(solution)/shard_map/ppermute | solution.py:35
  111.4 13.5 %copy-start.11 = (bf16[4096,128]{1,0:T(8,128)(2,1)S(1)}, bf16[4096,128]{1,0:T(8,128)(2,1)}, u32[]{:S(2)}) copy-start(bf16[4096,128]{1,0:T(8,128)(2,1)} %param.11) | copy-start | bytes 3145732
  111.4 10.1 %collective-permute-start.7 = (bf16[128,1408]{1,0:T(8,128)(2,1)S(1)}, bf16[128,1408]{1,0:T(8,128)(2,1)S(1)}, u32[]{:S(2)}, u32[]{:S(2)}) collective-permute-start(bf16[128,1408]{1,0:T(8,128)(2,1)S(1)} %pad_maximum_fusion.15), channel_id=1, source_target_pairs={{0,6},{1,7},{2,0},{3,1},{4,2},{5,3},{6,4},{7,5},{8,14},{9,15},{10,... | collective-permute-start | bytes 1081352 | tf_op jit(solution)/shard_map/ppermute | solution.py:35
  114.8 6.8 %copy-start.21 = (bf16[1024,4096]{1,0:T(8,128)(2,1)}, bf16[1024,4096]{1,0:T(8,128)(2,1)S(1)}, u32[]{:S(2)}) copy-start(bf16[1024,4096]{1,0:T(8,128)(2,1)S(1)} %constant_dynamic-update-slice_fusion.9) | copy-start | bytes 25165828
  115.0 12.2 %copy-start.6 = (bf16[4096,256]{1,0:T(8,128)(2,1)S(1)}, bf16[4096,256]{1,0:T(8,128)(2,1)}, u32[]{:S(2)}) copy-start(bf16[4096,256]{1,0:T(8,128)(2,1)} %param.10) | copy-start | bytes 6291460
  119.8 19.2 %collective-permute-start.24 = (bf16[128,1408]{1,0:T(8,128)(2,1)S(1)}, bf16[128,1408]{1,0:T(8,128)(2,1)S(1)}, u32[]{:S(2)}, u32[]{:S(2)}) collective-permute-start(bf16[128,1408]{1,0:T(8,128)(2,1)S(1)} %pad_maximum_fusion.14), channel_id=1, source_target_pairs={{0,1},{1,0},{2,3},{3,2},{4,5},{5,4},{6,7},{7,6},{8,9},{9,8},{10,11... | collective-permute-start | bytes 1081352 | tf_op jit(solution)/shard_map/ppermute | solution.py:35
  127.2 14.3 %copy-start.18 = (bf16[1024,128,1]{1,0,2:T(8,128)(2,1)}, bf16[1024,128,1]{1,0,2:T(8,128)(2,1)S(1)}, u32[]{:S(2)}) copy-start(bf16[1024,128,1]{1,0,2:T(8,128)(2,1)S(1)} %fusion.50) | copy-start | bytes 786436
  127.2 5.9 %copy-start.10 = (bf16[4096,128]{1,0:T(8,128)(2,1)S(1)}, bf16[4096,128]{1,0:T(8,128)(2,1)}, u32[]{:S(2)}) copy-start(bf16[4096,128]{1,0:T(8,128)(2,1)} %param.12) | copy-start | bytes 3145732
  133.1 5.9 %copy-start.22 = (bf16[1024,4096]{1,0:T(8,128)(2,1)S(1)}, bf16[1024,4096]{1,0:T(8,128)(2,1)}, u32[]{:S(2)}) copy-start(bf16[1024,4096]{1,0:T(8,128)(2,1)} %copy-done.21) | copy-start | bytes 25165828
  139.2 6.3 %copy-start.23 = (bf16[1024,4096]{1,0:T(8,128)(2,1)}, bf16[1024,4096]{1,0:T(8,128)(2,1)S(1)}, u32[]{:S(2)}) copy-start(bf16[1024,4096]{1,0:T(8,128)(2,1)S(1)} %maximum_dynamic-update-slice_fusion.1) | copy-start | bytes 25165828
  155.6 13.4 %copy-start.19 = (bf16[1024,128,1]{1,0,2:T(8,128)(2,1)S(1)}, bf16[1024,128,1]{1,0,2:T(8,128)(2,1)}, u32[]{:S(2)}) copy-start(bf16[1024,128,1]{1,0,2:T(8,128)(2,1)} %copy-done.18) | copy-start | bytes 786436
  169.7 15.6 %slice-start.6 = ((s8[8388608]{0:T(1024)(128)(4,1)}), s8[4194304]{0:T(1024)(128)(4,1)S(1)}, s32[]{:S(2)}) async-start(s8[8388608]{0:T(1024)(128)(4,1)} %bitcast.189), calls=%async_computation.8 | async-start | bytes 8388608
  177.0 8.2 %slice-start.7 = ((s8[8388608]{0:T(1024)(128)(4,1)}), s8[4194304]{0:T(1024)(128)(4,1)S(1)}, s32[]{:S(2)}) async-start(s8[8388608]{0:T(1024)(128)(4,1)} %bitcast.189), calls=%async_computation.9 | async-start | bytes 8388608
  221.7 7.5 %copy-start.15 = (bf16[128,2,1024]{2,0,1:T(8,128)(2,1)S(1)}, bf16[128,2,1024]{2,0,1:T(8,128)(2,1)}, u32[]{:S(2)}) copy-start(bf16[128,2,1024]{2,0,1:T(8,128)(2,1)} %fusion.35) | copy-start | bytes 1572868
  243.1 5.0 %copy-start.13 = (bf16[4096,128]{1,0:T(8,128)(2,1)S(1)}, bf16[4096,128]{1,0:T(8,128)(2,1)}, u32[]{:S(2)}) copy-start(bf16[4096,128]{1,0:T(8,128)(2,1)} %convolution_convert_fusion.4) | copy-start | bytes 3145732
  243.1 5.3 %copy-start.14 = (bf16[4096,128]{1,0:T(8,128)(2,1)S(1)}, bf16[4096,128]{1,0:T(8,128)(2,1)}, u32[]{:S(2)}) copy-start(bf16[4096,128]{1,0:T(8,128)(2,1)} %convolution_convert_fusion.3) | copy-start | bytes 3145732
  251.5 9.6 %collective-permute-start.28 = (bf16[128,1280]{1,0:T(8,128)(2,1)}, bf16[128,1280]{1,0:T(8,128)(2,1)S(1)}, u32[]{:S(2)}, u32[]{:S(2)}) collective-permute-start(bf16[128,1280]{1,0:T(8,128)(2,1)} %get-tuple-element.26), channel_id=1, source_target_pairs={{0,6},{1,7},{2,0},{3,1},{4,2},{5,3},{6,4},{7,5},{8,14},{9,15},{10,... | collective-permute-start | bytes 983048 | tf_op jit(solution)/shard_map/ppermute | solution.py:35
  253.4 12.6 %collective-permute-start.30 = (bf16[128,1408]{1,0:T(8,128)(2,1)}, bf16[128,1408]{1,0:T(8,128)(2,1)S(1)}, u32[]{:S(2)}, u32[]{:S(2)}) collective-permute-start(bf16[128,1408]{1,0:T(8,128)(2,1)} %get-tuple-element.23), channel_id=1, source_target_pairs={{0,1},{1,0},{2,3},{3,2},{4,5},{5,4},{6,7},{7,6},{8,9},{9,8},{10,11... | collective-permute-start | bytes 1081352 | tf_op jit(solution)/shard_map/ppermute | solution.py:35
  253.5 12.4 %collective-permute-start.27 = (bf16[128,1408]{1,0:T(8,128)(2,1)}, bf16[128,1408]{1,0:T(8,128)(2,1)S(1)}, u32[]{:S(2)}, u32[]{:S(2)}) collective-permute-start(bf16[128,1408]{1,0:T(8,128)(2,1)} %get-tuple-element.24), channel_id=1, source_target_pairs={{0,2},{1,3},{2,4},{3,5},{4,6},{5,7},{6,0},{7,1},{8,10},{9,11},{10,... | collective-permute-start | bytes 1081352 | tf_op jit(solution)/shard_map/ppermute | solution.py:35
  254.2 10.4 %collective-permute-start.10 = (bf16[128,1280]{1,0:T(8,128)(2,1)}, bf16[128,1280]{1,0:T(8,128)(2,1)S(1)}, u32[]{:S(2)}, u32[]{:S(2)}) collective-permute-start(bf16[128,1280]{1,0:T(8,128)(2,1)} %get-tuple-element.31), channel_id=1, source_target_pairs={{0,6},{1,7},{2,0},{3,1},{4,2},{5,3},{6,4},{7,5},{8,14},{9,15},{10,... | collective-permute-start | bytes 983048 | tf_op jit(solution)/shard_map/ppermute | solution.py:35
  258.1 13.8 %collective-permute-start.12 = (bf16[128,1408]{1,0:T(8,128)(2,1)S(1)}, bf16[128,1408]{1,0:T(8,128)(2,1)S(1)}, u32[]{:S(2)}, u32[]{:S(2)}) collective-permute-start(bf16[128,1408]{1,0:T(8,128)(2,1)S(1)} %get-tuple-element.28), channel_id=1, source_target_pairs={{0,1},{1,0},{2,3},{3,2},{4,5},{5,4},{6,7},{7,6},{8,9},{9,8},{10,11... | collective-permute-start | bytes 1081352 | tf_op jit(solution)/shard_map/ppermute | solution.py:35
  261.0 10.8 %collective-permute-start.9 = (bf16[128,1408]{1,0:T(8,128)(2,1)S(1)}, bf16[128,1408]{1,0:T(8,128)(2,1)S(1)}, u32[]{:S(2)}, u32[]{:S(2)}) collective-permute-start(bf16[128,1408]{1,0:T(8,128)(2,1)S(1)} %get-tuple-element.29), channel_id=1, source_target_pairs={{0,2},{1,3},{2,4},{3,5},{4,6},{5,7},{6,0},{7,1},{8,10},{9,11},{10,... | collective-permute-start | bytes 1081352 | tf_op jit(solution)/shard_map/ppermute | solution.py:35
  262.3 5.3 %copy-start.4 = (bf16[128,2688]{1,0:T(8,128)(2,1)S(1)}, bf16[128,2688]{1,0:T(8,128)(2,1)}, u32[]{:S(2)}) copy-start(bf16[128,2688]{1,0:T(8,128)(2,1)} %slice.456) | copy-start | bytes 2064388
  262.3 5.3 %copy-start.7 = (bf16[128,1408]{1,0:T(8,128)(2,1)S(1)}, bf16[128,1408]{1,0:T(8,128)(2,1)}, u32[]{:S(2)}) copy-start(bf16[128,1408]{1,0:T(8,128)(2,1)} %get-tuple-element.22) | copy-start | bytes 1081348
  262.3 5.3 %copy-start.9 = (bf16[128,1280]{1,0:T(8,128)(2,1)S(1)}, bf16[128,1280]{1,0:T(8,128)(2,1)}, u32[]{:S(2)}) copy-start(bf16[128,1280]{1,0:T(8,128)(2,1)} %get-tuple-element.25) | copy-start | bytes 983044
  267.8 6.1 %copy-start.3 = (bf16[128,2688]{1,0:T(8,128)(2,1)S(1)}, bf16[128,2688]{1,0:T(8,128)(2,1)}, u32[]{:S(2)}) copy-start(bf16[128,2688]{1,0:T(8,128)(2,1)} %slice.418) | copy-start | bytes 2064388
  267.9 6.1 %copy-start.8 = (bf16[128,1280]{1,0:T(8,128)(2,1)S(1)}, bf16[128,1280]{1,0:T(8,128)(2,1)}, u32[]{:S(2)}) copy-start(bf16[128,1280]{1,0:T(8,128)(2,1)} %get-tuple-element.30) | copy-start | bytes 983044
  268.1 26.1 %collective-permute-start.31 = (bf16[128,4096]{1,0:T(8,128)(2,1)S(1)}, bf16[128,4096]{1,0:T(8,128)(2,1)S(1)}, u32[]{:S(2)}, u32[]{:S(2)}) collective-permute-start(bf16[128,4096]{1,0:T(8,128)(2,1)S(1)} %pad_maximum_fusion.11), channel_id=1, source_target_pairs={{0,6},{1,7},{2,0},{3,1},{4,2},{5,3},{6,4},{7,5},{8,14},{9,15},{10,... | collective-permute-start | bytes 3145736 | tf_op jit(solution)/shard_map/ppermute | solution.py:35
  270.4 27.6 %collective-permute-start.33 = (bf16[128,4096]{1,0:T(8,128)(2,1)S(1)}, bf16[128,4096]{1,0:T(8,128)(2,1)S(1)}, u32[]{:S(2)}, u32[]{:S(2)}) collective-permute-start(bf16[128,4096]{1,0:T(8,128)(2,1)S(1)} %pad_maximum_fusion.12), channel_id=1, source_target_pairs={{0,2},{1,3},{2,4},{3,5},{4,6},{5,7},{6,0},{7,1},{8,10},{9,11},{10,... | collective-permute-start | bytes 3145736 | tf_op jit(solution)/shard_map/ppermute | solution.py:35
  270.8 31.1 %slice-start = ((s8[16777216]{0:T(1024)(128)(4,1)}), s8[4194304]{0:T(1024)(128)(4,1)S(1)}, s32[]{:S(2)}) async-start(s8[16777216]{0:T(1024)(128)(4,1)} %bitcast.169), calls=%async_computation.2 | async-start | bytes 8388608
  270.8 30.8 %collective-permute-start.29 = (bf16[128,4096]{1,0:T(8,128)(2,1)S(1)}, bf16[128,4096]{1,0:T(8,128)(2,1)S(1)}, u32[]{:S(2)}, u32[]{:S(2)}) collective-permute-start(bf16[128,4096]{1,0:T(8,128)(2,1)S(1)} %pad_maximum_fusion.10), channel_id=1, source_target_pairs={{0,1},{1,0},{2,3},{3,2},{4,5},{5,4},{6,7},{7,6},{8,9},{9,8},{10,11... | collective-permute-start | bytes 3145736 | tf_op jit(solution)/shard_map/ppermute | solution.py:35
  274.0 27.9 %slice-start.1 = ((s8[16777216]{0:T(1024)(128)(4,1)}), s8[4194304]{0:T(1024)(128)(4,1)S(1)}, s32[]{:S(2)}) async-start(s8[16777216]{0:T(1024)(128)(4,1)} %bitcast.169), calls=%async_computation.3 | async-start | bytes 8388608
  274.5 42.2 %collective-permute-start.13 = (bf16[128,4096]{1,0:T(8,128)(2,1)S(1)}, bf16[128,4096]{1,0:T(8,128)(2,1)S(1)}, u32[]{:S(2)}, u32[]{:S(2)}) collective-permute-start(bf16[128,4096]{1,0:T(8,128)(2,1)S(1)} %pad_maximum_fusion.5), channel_id=1, source_target_pairs={{0,6},{1,7},{2,0},{3,1},{4,2},{5,3},{6,4},{7,5},{8,14},{9,15},{10,... | collective-permute-start | bytes 3145736 | tf_op jit(solution)/shard_map/ppermute | solution.py:35
  277.8 24.0 %slice-start.2 = ((s8[16777216]{0:T(1024)(128)(4,1)}), s8[4194304]{0:T(1024)(128)(4,1)S(1)}, s32[]{:S(2)}) async-start(s8[16777216]{0:T(1024)(128)(4,1)} %bitcast.169), calls=%async_computation.4 | async-start | bytes 8388608
  277.9 42.0 %collective-permute-start.15 = (bf16[128,4096]{1,0:T(8,128)(2,1)S(1)}, bf16[128,4096]{1,0:T(8,128)(2,1)S(1)}, u32[]{:S(2)}, u32[]{:S(2)}) collective-permute-start(bf16[128,4096]{1,0:T(8,128)(2,1)S(1)} %pad_maximum_fusion.6), channel_id=1, source_target_pairs={{0,2},{1,3},{2,4},{3,5},{4,6},{5,7},{6,0},{7,1},{8,10},{9,11},{10,... | collective-permute-start | bytes 3145736 | tf_op jit(solution)/shard_map/ppermute | solution.py:35
  294.2 40.6 %collective-permute-start.11 = (bf16[128,4096]{1,0:T(8,128)(2,1)S(1)}, bf16[128,4096]{1,0:T(8,128)(2,1)S(1)}, u32[]{:S(2)}, u32[]{:S(2)}) collective-permute-start(bf16[128,4096]{1,0:T(8,128)(2,1)S(1)} %pad_maximum_fusion.4), channel_id=1, source_target_pairs={{0,1},{1,0},{2,3},{3,2},{4,5},{5,4},{6,7},{7,6},{8,9},{9,8},{10,11... | collective-permute-start | bytes 3145736 | tf_op jit(solution)/shard_map/ppermute | solution.py:35
  295.4 6.4 %slice-start.3 = ((s8[16777216]{0:T(1024)(128)(4,1)}), s8[4194304]{0:T(1024)(128)(4,1)S(1)}, s32[]{:S(2)}) async-start(s8[16777216]{0:T(1024)(128)(4,1)} %bitcast.169), calls=%async_computation.5 | async-start | bytes 8388608
  302.7 41.1 %collective-permute-start.32 = (bf16[128,4096]{1,0:T(8,128)(2,1)S(1)}, bf16[128,4096]{1,0:T(8,128)(2,1)S(1)}, u32[]{:S(2)}, u32[]{:S(2)}) collective-permute-start(bf16[128,4096]{1,0:T(8,128)(2,1)S(1)} %get-tuple-element.12), channel_id=1, source_target_pairs={{0,6},{1,7},{2,0},{3,1},{4,2},{5,3},{6,4},{7,5},{8,14},{9,15},{10,... | collective-permute-start | bytes 3145736 | tf_op jit(solution)/shard_map/ppermute | solution.py:35
  305.8 55.8 %collective-permute-start.35 = (bf16[128,4096]{1,0:T(8,128)(2,1)S(1)}, bf16[128,4096]{1,0:T(8,128)(2,1)S(1)}, u32[]{:S(2)}, u32[]{:S(2)}) collective-permute-start(bf16[128,4096]{1,0:T(8,128)(2,1)S(1)} %get-tuple-element.13), channel_id=1, source_target_pairs={{0,1},{1,0},{2,3},{3,2},{4,5},{5,4},{6,7},{7,6},{8,9},{9,8},{10,11... | collective-permute-start | bytes 3145736 | tf_op jit(solution)/shard_map/ppermute | solution.py:35
  316.7 44.8 %collective-permute-start.34 = (bf16[128,4096]{1,0:T(8,128)(2,1)S(1)}, bf16[128,4096]{1,0:T(8,128)(2,1)S(1)}, u32[]{:S(2)}, u32[]{:S(2)}) collective-permute-start(bf16[128,4096]{1,0:T(8,128)(2,1)S(1)} %get-tuple-element.14), channel_id=1, source_target_pairs={{0,2},{1,3},{2,4},{3,5},{4,6},{5,7},{6,0},{7,1},{8,10},{9,11},{10,... | collective-permute-start | bytes 3145736 | tf_op jit(solution)/shard_map/ppermute | solution.py:35
  335.1 26.5 %copy-start.1 = (bf16[1,128,4096]{2,1,0:T(8,128)(2,1)S(1)}, bf16[1,128,4096]{2,1,0:T(8,128)(2,1)}, u32[]{:S(2)}) copy-start(bf16[1,128,4096]{2,1,0:T(8,128)(2,1)} %param.8) | copy-start | bytes 3145732
  335.1 26.5 %copy-start.17 = (f32[4096]{0:T(1024)S(1)}, f32[4096]{0:T(1024)}, u32[]{:S(2)}) copy-start(f32[4096]{0:T(1024)} %copy-done.16) | copy-start | bytes 49156
  335.1 26.5 %copy-start.25 = (f32[128]{0:T(128)S(1)}, f32[128]{0:T(128)}, u32[]{:S(2)}) copy-start(f32[128]{0:T(128)} %copy-done.24) | copy-start | bytes 1540
  339.5 96.7 %collective-permute-start.14 = (bf16[128,4096]{1,0:T(8,128)(2,1)}, bf16[128,4096]{1,0:T(8,128)(2,1)}, u32[]{:S(2)}, u32[]{:S(2)}) collective-permute-start(bf16[128,4096]{1,0:T(8,128)(2,1)} %get-tuple-element.17), channel_id=1, source_target_pairs={{0,6},{1,7},{2,0},{3,1},{4,2},{5,3},{6,4},{7,5},{8,14},{9,15},{10,... | collective-permute-start | bytes 3145736 | tf_op jit(solution)/shard_map/ppermute | solution.py:35
  342.2 94.0 %collective-permute-start.17 = (bf16[128,4096]{1,0:T(8,128)(2,1)}, bf16[128,4096]{1,0:T(8,128)(2,1)}, u32[]{:S(2)}, u32[]{:S(2)}) collective-permute-start(bf16[128,4096]{1,0:T(8,128)(2,1)} %get-tuple-element.18), channel_id=1, source_target_pairs={{0,1},{1,0},{2,3},{3,2},{4,5},{5,4},{6,7},{7,6},{8,9},{9,8},{10,11... | collective-permute-start | bytes 3145736 | tf_op jit(solution)/shard_map/ppermute | solution.py:35
  343.8 92.4 %collective-permute-start.16 = (bf16[128,4096]{1,0:T(8,128)(2,1)}, bf16[128,4096]{1,0:T(8,128)(2,1)}, u32[]{:S(2)}, u32[]{:S(2)}) collective-permute-start(bf16[128,4096]{1,0:T(8,128)(2,1)} %get-tuple-element.19), channel_id=1, source_target_pairs={{0,2},{1,3},{2,4},{3,5},{4,6},{5,7},{6,0},{7,1},{8,10},{9,11},{10,... | collective-permute-start | bytes 3145736 | tf_op jit(solution)/shard_map/ppermute | solution.py:35
  (7 other events, 24.4 us)
Sparse Core Ops, SparseCore 0:
  251.6 111.5 reduce-scatter.1

commit v2 on v1

--- a/solution.py
+++ b/solution.py
@@ -92,6 +92,23 @@
     return me + from_a + from_b + from_c
 
 
+def _dp_perm(fn):
+    return [(d, fn(d)) for d in range(DP_SIZE)]
+
+
+DP_SIZE = 16
+DP_XOR = (1, 2, 4, 8)
+T_XOR = (1, 2, 4)
+
+
+def butterfly_sum(v):
+    for k in DP_XOR:
+        v = v + lax.ppermute(v, "dp", _dp_perm(lambda d, k=k: d ^ k))
+    for k in T_XOR:
+        v = v + _pp(v, _perm(lambda t, k=k: t ^ k))
+    return v
+
+
 def per_device(
     layer_input, norm_gain, w_query, w_key, value_weight, w_out, prefix_len, grad_output
 ):
@@ -105,8 +122,8 @@
     inv_rms = lax.rsqrt(jnp.mean(rows_f * rows_f, axis=1, keepdims=True) + EPS)
     unit_rows = rows_f * inv_rms
     normed = (unit_rows * gain_vec).astype(jnp.bfloat16)
-    grad_local = grad_output[0]
     full_normed = gather_tensor(normed)
+    full_normed, grad_local = lax.optimization_barrier((full_normed, grad_output[0]))
     full_grad = gather_tensor(grad_local)
     sequence_length = full_normed.shape[0]
 
@@ -234,7 +251,7 @@
     sum_k = reduced[:, wq_cols:wq_cols + wk_cols]
     sum_v = reduced[:, wq_cols + wk_cols:wq_cols + wk_cols + wv_cols]
     grad_wout = reduced[:, wq_cols + wk_cols + wv_cols:]
-    grad_gain = lax.psum(gain_term, ("dp", "tensor"))
+    grad_gain = butterfly_sum(gain_term)
     return (
         layer_output,
         grad_input,

time: 462 us -> 411 us (0.89)
  blocking collectives: 72.5 us -> 0 us
  waiting for transfers between devices: 132 us -> 155 us
  local copies, waits for them, and re-layouts: 36.1 us -> 48.6 us
  matrix products: 96.5 us -> 86 us
  starting transfers between devices: 54 us -> 59.5 us
  other arithmetic: 45 us -> 39.6 us
    psum x1 -> x0, blocking collectives: 72.5 us -> none  [per_device(): grad_gain = lax.psum(gain_term, ('dp', 'tensor'))]
    ppermute x36 -> x39, waiting for transfers between devices: 132 us -> 145 us  [_pp(): return lax.ppermute(x, 'tensor', perm)]
    ppermute x0 -> x4, waiting for transfers between devices: none -> 10.4 us  [butterfly_sum(): v = v + lax.ppermute(v, 'dp', _dp_perm(lambda d, k=k: d ^ k))]
    another operation x5, other arithmetic: 12.5 us -> 3.97 us
    ppermute x0 -> x4, starting transfers between devices: none -> 8.53 us  [butterfly_sum(): v = v + lax.ppermute(v, 'dp', _dp_perm(lambda d, k=k: d ^ k))]
    slice x4, local copies, waits for them, and re-layouts: 0.81 us -> 7.24 us  [scatter_tensor(): a = a + jnp.concatenate([s_z[h:], s_ym[:h]], 0)]
    ppermute x36 -> x39, starting transfers between devices: 54 us -> 50.9 us  [_pp(): return lax.ppermute(x, 'tensor', perm)]
    unnamed x81 -> x89, local copies, waits for them, and re-layouts: 14.2 us -> 11.5 us
  transfers between devices with their start and end apart: 37 -> 44, of which waited for: 17 -> 26; matrix products, arithmetic and copies ran while one was open for 13% -> 40% of each run, Pallas kernels for 0% -> 0%
where the time goes in v2:
time: 411 us; the launch traced here: 405 us
  waiting for transfers between devices  155 us (38%)
  matrix products  86 us (21%)
  starting transfers between devices  59.5 us (14%)
  local copies, waits for them, and re-layouts  48.6 us (12%)
  other arithmetic  39.6 us (10%)
  between operations  16 us (4%)
    ppermute x39, waiting for transfers between devices, _pp(): return lax.ppermute(x, 'tensor', perm)  145 us
    ppermute x39, starting transfers between devices, _pp(): return lax.ppermute(x, 'tensor', perm)  50.9 us
    dot_general x1, matrix products, per_device(): jnp.einsum('sh,dh->sd', value_gradient, value_weight, preferred_element_t...  20.9 us
    unnamed x89, local copies, waits for them, and re-layouts  11.5 us
    ppermute x4, waiting for transfers between devices, butterfly_sum(): v = v + lax.ppermute(v, 'dp', _dp_perm(lambda d, k=k: d ^ k))  10.4 us
    ppermute x4, starting transfers between devices, butterfly_sum(): v = v + lax.ppermute(v, 'dp', _dp_perm(lambda d, k=k: d ^ k))  8.53 us
  transfers between devices with their start and end apart: 44, of which 26 were waited for; matrix products, arithmetic and copies ran while one was open for 40% of the time, Pallas kernels for 0%

profile of v2, /device:TPU:0, one launch (start us, length us, event | category | flops | bytes accessed | tf_op | source)
XLA Modules:
  0.0 404.8 jit_solution(11220460737568486941)
XLA Ops:
  10.2 3.0 constant_dynamic-update-slice_fusion.8
  13.2 2.0 collective-permute-start.2
  15.2 3.0 collective-permute-start.1
  20.1 18.6 %collective-permute-done.2 = bf16[128,4096]{1,0:T(8,128)(2,1)} collective-permute-done((bf16[128,4096]{1,0:T(8,128)(2,1)}, bf16[128,4096]{1,0:T(8,128)(2,1)}, u32[]{:S(2)}, u32[]{:S(2)}) %collective-permute-start.2) | collective-permute-done | bytes 1048608 | tf_op jit(solution)/shard_map/ppermute | solution.py:35
  42.1 3.8 collective-permute-start.3
  51.8 15.3 %collective-permute-done.3 = bf16[128,4096]{1,0:T(8,128)(2,1)S(1)} collective-permute-done((bf16[128,4096]{1,0:T(8,128)(2,1)S(1)}, bf16[128,4096]{1,0:T(8,128)(2,1)S(1)}, u32[]{:S(2)}, u32[]{:S(2)}) %collective-permute-start.3) | collective-permute-done | bytes 1048608 | tf_op jit(solution)/shard_map/ppermute | solution.py:35
  67.3 4.7 %collective-permute-done.4 = bf16[128,4096]{1,0:T(8,128)(2,1)S(1)} collective-permute-done((bf16[128,4096]{1,0:T(8,128)(2,1)S(1)}, bf16[128,4096]{1,0:T(8,128)(2,1)S(1)}, u32[]{:S(2)}, u32[]{:S(2)}) %collective-permute-start.4) | collective-permute-done | bytes 1048608 | tf_op jit(solution)/shard_map/ppermute | solution.py:35
  73.1 3.3 collective-permute-start.7
  76.6 4.9 %collective-permute-done.8 = bf16[128,1280]{1,0:T(8,128)(2,1)S(1)} collective-permute-done((bf16[128,1280]{1,0:T(8,128)(2,1)S(1)}, bf16[128,1280]{1,0:T(8,128)(2,1)S(1)}, u32[]{:S(2)}, u32[]{:S(2)}) %collective-permute-start.8) | collective-permute-done | bytes 327712 | tf_op jit(solution)/shard_map/ppermute | solution.py:35
  83.0 3.7 collective-permute-start.19
  86.8 2.3 fusion.50
  89.2 2.3 fusion.49
  91.5 2.4 convolution_convert_fusion.6
  94.0 1.9 fusion.6
  95.8 2.2 fusion.5
  98.1 3.7 fusion.35
  101.8 6.8 %fusion.88 = (f32[1024,4096]{1,0:T(8,128)S(1)}, bf16[1024,4096]{1,0:T(8,128)(2,1)}) fusion(bf16[1024,256]{0,1:T(8,128)(2,1)} %bitcast.180, bf16[256,4096]{1,0:T(8,128)(2,1)S(1)} %copy-done), kind=kOutput, calls=%fused_computation.161 | convolution fusion | flops 2155872256 | bytes 27787264 | tf_op jit(solution)/shard_map/dot_general | solution.py:167
  113.5 2.1 fusion.59
  115.6 3.3 collective-permute-start.10
  121.0 2.5 collective-permute-done.10
  123.7 2.6 collective-permute-done.12
  126.3 7.1 %collective-permute-done.9 = bf16[128,1408]{1,0:T(8,128)(2,1)S(1)} collective-permute-done((bf16[128,1408]{1,0:T(8,128)(2,1)S(1)}, bf16[128,1408]{1,0:T(8,128)(2,1)S(1)}, u32[]{:S(2)}, u32[]{:S(2)}) %collective-permute-start.9) | collective-permute-done | bytes 360480 | tf_op jit(solution)/shard_map/ppermute | solution.py:35
  134.1 5.0 %collective-permute-start.13 = (bf16[128,4096]{1,0:T(8,128)(2,1)S(1)}, bf16[128,4096]{1,0:T(8,128)(2,1)S(1)}, u32[]{:S(2)}, u32[]{:S(2)}) collective-permute-start(bf16[128,4096]{1,0:T(8,128)(2,1)S(1)} %pad_maximum_fusion.5), channel_id=1, source_target_pairs={{0,6},{1,7},{2,0},{3,1},{4,2},{5,3},{6,4},{7,5},{8,14},{9,15},{10,... | collective-permute-start | bytes 3145736 | tf_op jit(solution)/shard_map/ppermute | solution.py:35
  143.3 3.3 collective-permute-start.21
  152.0 9.8 %collective-permute-done.13 = bf16[128,4096]{1,0:T(8,128)(2,1)S(1)} collective-permute-done((bf16[128,4096]{1,0:T(8,128)(2,1)S(1)}, bf16[128,4096]{1,0:T(8,128)(2,1)S(1)}, u32[]{:S(2)}, u32[]{:S(2)}) %collective-permute-start.13) | collective-permute-done | bytes 1048608 | tf_op jit(solution)/shard_map/ppermute | solution.py:35
  164.5 1.8 collective-permute-done.15
  167.8 9.3 %collective-permute-done.21 = bf16[128,4096]{1,0:T(8,128)(2,1)S(1)} collective-permute-done((bf16[128,4096]{1,0:T(8,128)(2,1)S(1)}, bf16[128,4096]{1,0:T(8,128)(2,1)S(1)}, u32[]{:S(2)}, u32[]{:S(2)}) %collective-permute-start.21) | collective-permute-done | bytes 1048608 | tf_op jit(solution)/shard_map/ppermute | solution.py:35
  177.3 4.4 %collective-permute-done.23 = bf16[128,4096]{1,0:T(8,128)(2,1)S(1)} collective-permute-done((bf16[128,4096]{1,0:T(8,128)(2,1)S(1)}, bf16[128,4096]{1,0:T(8,128)(2,1)S(1)}, u32[]{:S(2)}, u32[]{:S(2)}) %collective-permute-start.23) | collective-permute-done | bytes 1048608 | tf_op jit(solution)/shard_map/ppermute | solution.py:35
  181.8 2.7 collective-permute-start.25
  186.4 6.6 %collective-permute-done.26 = bf16[128,1280]{1,0:T(8,128)(2,1)S(1)} collective-permute-done((bf16[128,1280]{1,0:T(8,128)(2,1)S(1)}, bf16[128,1280]{1,0:T(8,128)(2,1)S(1)}, u32[]{:S(2)}, u32[]{:S(2)}) %collective-permute-start.26) | collective-permute-done | bytes 327712 | tf_op jit(solution)/shard_map/ppermute | solution.py:35
  193.1 2.4 convolution_convert_fusion.5
  195.5 3.7 convolution_convert_fusion.1
  199.2 3.0 fusion.45
  202.2 3.4 fusion
  205.6 3.3 fusion.7
  211.2 7.4 %convolution_convert_fusion.2 = bf16[4096,256]{1,0:T(8,128)(2,1)} fusion(bf16[1024,4096]{1,0:T(8,128)(2,1)} %copy-done.23, bf16[1024,256]{0,1:T(8,128)(2,1)S(1)} %bitcast.172), kind=kOutput, calls=%fused_computation.15 | convolution fusion | flops 2148532224 | bytes 11010048 | tf_op jit(solution)/shard_map/sd,sh->dh/dot_general | solution.py:223
  218.6 8.2 %fusion.89 = f32[1024,4096]{1,0:T(8,128)} fusion(bf16[1024,256]{0,1:T(8,128)(2,1)S(1)} %bitcast.173, bf16[4096,256]{1,0:T(8,128)(2,1)S(1)} %copy-done.8), kind=kOutput, calls=%fused_computation.162 | convolution fusion | flops 2147483648 | bytes 19398656 | tf_op jit(solution)/shard_map/sh,dh->sd/dot_general | solution.py:208
  226.8 3.5 convolution_convert_fusion.4
  230.2 8.2 %fusion.90 = f32[1024,4096]{1,0:T(8,128)} fusion(bf16[1024,128]{0,1:T(8,128)(2,1)S(1)} %fusion.48, bf16[4096,128]{1,0:T(8,128)(2,1)S(1)} %copy-done.13), kind=kOutput, calls=%fused_computation.163 | convolution fusion | flops 1073741824 | bytes 18087936 | tf_op jit(solution)/shard_map/sh,dh->sd/dot_general | solution.py:209
  238.4 3.7 convolution_convert_fusion.3
  242.1 20.9 %fusion.87 = (f32[1024,4096]{1,0:T(8,128)}, bf16[1024,4096]{1,0:T(8,128)(2,1)}) fusion(bf16[1024,128]{0,1:T(8,128)(2,1)S(1)} %fusion.45, bf16[4096,128]{1,0:T(8,128)(2,1)S(1)} %copy-done.11, f32[1024,4096]{1,0:T(8,128)} %fusion.89, f32[1024,4096]{1,0:T(8,128)} %fusion.90), kind=kOutput, calls=%fused_computation.160 | convolution fusion | flops 1090519040 | bytes 60030976 | tf_op jit(solution)/shard_map/sh,dh->sd/dot_general | solution.py:212
  263.1 2.2 fusion.58
  269.4 3.2 pad_maximum_fusion
  273.5 2.9 collective-permute-start.28
  278.8 5.7 %collective-permute-done.28 = bf16[128,1280]{1,0:T(8,128)(2,1)S(1)} collective-permute-done((bf16[128,1280]{1,0:T(8,128)(2,1)S(1)}, bf16[128,1280]{1,0:T(8,128)(2,1)S(1)}, u32[]{:S(2)}, u32[]{:S(2)}) %collective-permute-start.28) | collective-permute-done | bytes 327712 | tf_op jit(solution)/shard_map/ppermute | solution.py:35
  285.9 3.2 collective-permute-done.30
  289.0 2.2 collective-permute-done.27
  296.9 15.0 %collective-permute-done.31 = bf16[128,4096]{1,0:T(8,128)(2,1)S(1)} collective-permute-done((bf16[128,4096]{1,0:T(8,128)(2,1)S(1)}, bf16[128,4096]{1,0:T(8,128)(2,1)S(1)}, u32[]{:S(2)}, u32[]{:S(2)}) %collective-permute-start.31) | collective-permute-done | bytes 1048608 | tf_op jit(solution)/shard_map/ppermute | solution.py:35
  316.5 4.4 %fusion.27 = (bf16[128,4096]{1,0:T(8,128)(2,1)}, bf16[128,4096]{1,0:T(8,128)(2,1)}, bf16[128,4096]{1,0:T(8,128)(2,1)}) fusion(f32[1024,4096]{1,0:T(8,128)S(1)} %bitcast.168, f32[64,4096]{1,0:T(8,128)S(1)} %get-tuple-element.40, f32[64,4096]{1,0:T(8,128)} %get-tuple-element.38, f32[64,4096]{1,0:T(8,128)} %get-tuple-element.41, ...), kind=kLoop, calls=%fused_computation.46 | loop fusion | flops 4718592 | bytes 15728640 | tf_op jit(solution)/shard_map/convert_element_type | solution.py:89
  321.2 3.0 fusion.73
  324.2 2.1 collective-permute-start.35
  326.9 3.8 fusion.32
  330.7 2.7 collective-permute-start.14
  333.4 8.6 %collective-permute-done.32 = bf16[128,4096]{1,0:T(8,128)(2,1)} collective-permute-done((bf16[128,4096]{1,0:T(8,128)(2,1)}, bf16[128,4096]{1,0:T(8,128)(2,1)}, u32[]{:S(2)}, u32[]{:S(2)}) %collective-permute-start.32) | collective-permute-done | bytes 1048608 | tf_op jit(solution)/shard_map/ppermute | solution.py:35
  342.0 14.7 %collective-permute-done.35 = bf16[128,4096]{1,0:T(8,128)(2,1)} collective-permute-done((bf16[128,4096]{1,0:T(8,128)(2,1)}, bf16[128,4096]{1,0:T(8,128)(2,1)}, u32[]{:S(2)}, u32[]{:S(2)}) %collective-permute-start.35) | collective-permute-done | bytes 1048608 | tf_op jit(solution)/shard_map/ppermute | solution.py:35
  356.7 4.0 fusion.22
  363.6 2.3 collective-permute-done.37
  365.9 3.0 collective-permute-start.38
  368.9 2.2 collective-permute-done.38
  371.1 3.8 collective-permute-start.39
  374.9 4.7 %collective-permute-done.39 = f32[4096]{0:T(1024)S(1)} collective-permute-done((f32[4096]{0:T(1024)S(1)}, f32[4096]{0:T(1024)S(1)}, u32[]{:S(2)}, u32[]{:S(2)}) %collective-permute-start.39) | collective-permute-done | bytes 16416 | tf_op jit(solution)/shard_map/ppermute | solution.py:106
  380.1 3.3 collective-permute-done.40
  383.4 3.7 collective-permute-done.41
  388.2 5.6 %fusion.52 = (bf16[1,128,4096]{2,1,0:T(8,128)(2,1)}, bf16[1,128,4096]{2,1,0:T(8,128)(2,1)}) fusion(f32[128,4096]{1,0:T(8,128)} %get-tuple-element.13, bf16[128,4096]{1,0:T(8,128)(2,1)} %bitcast.2, bf16[1,128,4096]{2,1,0:T(8,128)(2,1)S(1)} %copy-done.3, f32[128]{0:T(128)S(1)} %broadcast_multiply_fusion.1, f32[4096]{0:T(1024)S(1)} %copy-done.19, ...), kind=kLoop, calls=%fused_computation.80 | loop fusion | flops 9437184 | bytes 11551744 | tf_op jit(solution)/shard_map/broadcast_in_dim | solution.py:217
  (222 shorter events, 70.9 us)
Async XLA Ops:
  7.2 94.6 %copy-start = (bf16[256,4096]{1,0:T(8,128)(2,1)S(1)}, bf16[256,4096]{1,0:T(8,128)(2,1)}, u32[]{:S(2)}) copy-start(bf16[256,4096]{1,0:T(8,128)(2,1)} %param.13) | copy-start | bytes 6291460
  7.2 387.2 %reduce-scatter.2.cloned.1.call-start = ((), (), s32[]{:S(2)}) async-start(), calls=%async_computation.1 | async-start | bytes 6684672 | tf_op jit(solution)/shard_map/reduce_scatter | solution.py:249
  13.2 25.5 %collective-permute-start.2 = (bf16[128,4096]{1,0:T(8,128)(2,1)}, bf16[128,4096]{1,0:T(8,128)(2,1)}, u32[]{:S(2)}, u32[]{:S(2)}) collective-permute-start(bf16[128,4096]{1,0:T(8,128)(2,1)} %get-tuple-element.15), channel_id=1, source_target_pairs={{0,1},{1,0},{2,3},{3,2},{4,5},{5,4},{6,7},{7,6},{8,9},{9,8},{10,11... | collective-permute-start | bytes 3145736 | tf_op jit(solution)/shard_map/ppermute | solution.py:35
  15.2 25.5 %collective-permute-start.1 = (bf16[128,4096]{1,0:T(8,128)(2,1)}, bf16[128,4096]{1,0:T(8,128)(2,1)}, u32[]{:S(2)}, u32[]{:S(2)}) collective-permute-start(bf16[128,4096]{1,0:T(8,128)(2,1)} %get-tuple-element.15), channel_id=1, source_target_pairs={{0,6},{1,7},{2,0},{3,1},{4,2},{5,3},{6,4},{7,5},{8,14},{9,15},{10,... | collective-permute-start | bytes 3145736 | tf_op jit(solution)/shard_map/ppermute | solution.py:35
  18.2 27.6 %collective-permute-start = (bf16[128,4096]{1,0:T(8,128)(2,1)}, bf16[128,4096]{1,0:T(8,128)(2,1)}, u32[]{:S(2)}, u32[]{:S(2)}) collective-permute-start(bf16[128,4096]{1,0:T(8,128)(2,1)} %get-tuple-element.15), channel_id=1, source_target_pairs={{0,2},{1,3},{2,4},{3,5},{4,6},{5,7},{6,0},{7,1},{8,10},{9,11},{10,... | collective-permute-start | bytes 3145736 | tf_op jit(solution)/shard_map/ppermute | solution.py:35
  20.1 27.7 %copy-start.22 = (bf16[1024,4096]{1,0:T(8,128)(2,1)S(1)}, bf16[1024,4096]{1,0:T(8,128)(2,1)}, u32[]{:S(2)}) copy-start(bf16[1024,4096]{1,0:T(8,128)(2,1)} %get-tuple-element.14) | copy-start | bytes 25165828
  42.1 25.0 %collective-permute-start.3 = (bf16[128,4096]{1,0:T(8,128)(2,1)S(1)}, bf16[128,4096]{1,0:T(8,128)(2,1)S(1)}, u32[]{:S(2)}, u32[]{:S(2)}) collective-permute-start(bf16[128,4096]{1,0:T(8,128)(2,1)S(1)} %pad_maximum_fusion.1), channel_id=1, source_target_pairs={{0,6},{1,7},{2,0},{3,1},{4,2},{5,3},{6,4},{7,5},{8,14},{9,15},{10,... | collective-permute-start | bytes 3145736 | tf_op jit(solution)/shard_map/ppermute | solution.py:35
  47.2 24.8 %collective-permute-start.4 = (bf16[128,4096]{1,0:T(8,128)(2,1)S(1)}, bf16[128,4096]{1,0:T(8,128)(2,1)S(1)}, u32[]{:S(2)}, u32[]{:S(2)}) collective-permute-start(bf16[128,4096]{1,0:T(8,128)(2,1)S(1)} %pad_maximum_fusion.2), channel_id=1, source_target_pairs={{0,2},{1,3},{2,4},{3,5},{4,6},{5,7},{6,0},{7,1},{8,10},{9,11},{10,... | collective-permute-start | bytes 3145736 | tf_op jit(solution)/shard_map/ppermute | solution.py:35
  47.4 25.5 %collective-permute-start.5 = (bf16[128,4096]{1,0:T(8,128)(2,1)S(1)}, bf16[128,4096]{1,0:T(8,128)(2,1)S(1)}, u32[]{:S(2)}, u32[]{:S(2)}) collective-permute-start(bf16[128,4096]{1,0:T(8,128)(2,1)S(1)} %pad_maximum_fusion.3), channel_id=1, source_target_pairs={{0,1},{1,0},{2,3},{3,2},{4,5},{5,4},{6,7},{7,6},{8,9},{9,8},{10,11... | collective-permute-start | bytes 3145736 | tf_op jit(solution)/shard_map/ppermute | solution.py:35
  72.1 14.7 %copy-start.12 = (bf16[4096,128]{1,0:T(8,128)(2,1)S(1)}, bf16[4096,128]{1,0:T(8,128)(2,1)}, u32[]{:S(2)}) copy-start(bf16[4096,128]{1,0:T(8,128)(2,1)} %param.11) | copy-start | bytes 3145732
  72.2 9.3 %collective-permute-start.6 = (bf16[128,1408]{1,0:T(8,128)(2,1)S(1)}, bf16[128,1408]{1,0:T(8,128)(2,1)S(1)}, u32[]{:S(2)}, u32[]{:S(2)}) collective-permute-start(bf16[128,1408]{1,0:T(8,128)(2,1)S(1)} %pad_maximum_fusion.16), channel_id=1, source_target_pairs={{0,1},{1,0},{2,3},{3,2},{4,5},{5,4},{6,7},{7,6},{8,9},{9,8},{10,11... | collective-permute-start | bytes 1081352 | tf_op jit(solution)/shard_map/ppermute | solution.py:35
  73.0 8.5 %collective-permute-start.8 = (bf16[128,1280]{1,0:T(8,128)(2,1)S(1)}, bf16[128,1280]{1,0:T(8,128)(2,1)S(1)}, u32[]{:S(2)}, u32[]{:S(2)}) collective-permute-start(bf16[128,1280]{1,0:T(8,128)(2,1)S(1)} %pad_maximum_fusion.18), channel_id=1, source_target_pairs={{0,2},{1,3},{2,4},{3,5},{4,6},{5,7},{6,0},{7,1},{8,10},{9,11},{10,... | collective-permute-start | bytes 983048 | tf_op jit(solution)/shard_map/ppermute | solution.py:35
  73.1 8.4 %collective-permute-start.7 = (bf16[128,1408]{1,0:T(8,128)(2,1)S(1)}, bf16[128,1408]{1,0:T(8,128)(2,1)S(1)}, u32[]{:S(2)}, u32[]{:S(2)}) collective-permute-start(bf16[128,1408]{1,0:T(8,128)(2,1)S(1)} %pad_maximum_fusion.15), channel_id=1, source_target_pairs={{0,6},{1,7},{2,0},{3,1},{4,2},{5,3},{6,4},{7,5},{8,14},{9,15},{10,... | collective-permute-start | bytes 1081352 | tf_op jit(solution)/shard_map/ppermute | solution.py:35
  76.6 12.6 %copy-start.10 = (bf16[4096,128]{1,0:T(8,128)(2,1)S(1)}, bf16[4096,128]{1,0:T(8,128)(2,1)}, u32[]{:S(2)}) copy-start(bf16[4096,128]{1,0:T(8,128)(2,1)} %param.12) | copy-start | bytes 3145732
  81.7 58.7 %collective-permute-start.20 = (bf16[128,4096]{1,0:T(8,128)(2,1)}, bf16[128,4096]{1,0:T(8,128)(2,1)}, u32[]{:S(2)}, u32[]{:S(2)}) collective-permute-start(bf16[128,4096]{1,0:T(8,128)(2,1)} %bitcast.2), channel_id=1, source_target_pairs={{0,1},{1,0},{2,3},{3,2},{4,5},{5,4},{6,7},{7,6},{8,9},{9,8},{10,11... | collective-permute-start | bytes 3145736 | tf_op jit(solution)/shard_map/ppermute | solution.py:35
  83.0 58.9 %collective-permute-start.19 = (bf16[128,4096]{1,0:T(8,128)(2,1)}, bf16[128,4096]{1,0:T(8,128)(2,1)}, u32[]{:S(2)}, u32[]{:S(2)}) collective-permute-start(bf16[128,4096]{1,0:T(8,128)(2,1)} %bitcast.2), channel_id=1, source_target_pairs={{0,6},{1,7},{2,0},{3,1},{4,2},{5,3},{6,4},{7,5},{8,14},{9,15},{10,... | collective-permute-start | bytes 3145736 | tf_op jit(solution)/shard_map/ppermute | solution.py:35
  86.6 59.9 %collective-permute-start.18 = (bf16[128,4096]{1,0:T(8,128)(2,1)}, bf16[128,4096]{1,0:T(8,128)(2,1)}, u32[]{:S(2)}, u32[]{:S(2)}) collective-permute-start(bf16[128,4096]{1,0:T(8,128)(2,1)} %bitcast.2), channel_id=1, source_target_pairs={{0,2},{1,3},{2,4},{3,5},{4,6},{5,7},{6,0},{7,1},{8,10},{9,11},{10,... | collective-permute-start | bytes 3145736 | tf_op jit(solution)/shard_map/ppermute | solution.py:35
  108.6 34.7 %copy-start.2 = (f32[1024,4096]{1,0:T(8,128)}, f32[1024,4096]{1,0:T(8,128)S(1)}, u32[]{:S(2)}) copy-start(f32[1024,4096]{1,0:T(8,128)S(1)} %get-tuple-element.100) | copy-start | bytes 50331652
  115.6 7.9 %collective-permute-start.10 = (bf16[128,1280]{1,0:T(8,128)(2,1)S(1)}, bf16[128,1280]{1,0:T(8,128)(2,1)S(1)}, u32[]{:S(2)}, u32[]{:S(2)}) collective-permute-start(bf16[128,1280]{1,0:T(8,128)(2,1)S(1)} %get-tuple-element.35), channel_id=1, source_target_pairs={{0,6},{1,7},{2,0},{3,1},{4,2},{5,3},{6,4},{7,5},{8,14},{9,15},{10,... | collective-permute-start | bytes 983048 | tf_op jit(solution)/shard_map/ppermute | solution.py:35
  118.9 7.4 %collective-permute-start.12 = (bf16[128,1408]{1,0:T(8,128)(2,1)S(1)}, bf16[128,1408]{1,0:T(8,128)(2,1)S(1)}, u32[]{:S(2)}, u32[]{:S(2)}) collective-permute-start(bf16[128,1408]{1,0:T(8,128)(2,1)S(1)} %get-tuple-element.32), channel_id=1, source_target_pairs={{0,1},{1,0},{2,3},{3,2},{4,5},{5,4},{6,7},{7,6},{8,9},{9,8},{10,11... | collective-permute-start | bytes 1081352 | tf_op jit(solution)/shard_map/ppermute | solution.py:35
  123.5 9.9 %collective-permute-start.9 = (bf16[128,1408]{1,0:T(8,128)(2,1)S(1)}, bf16[128,1408]{1,0:T(8,128)(2,1)S(1)}, u32[]{:S(2)}, u32[]{:S(2)}) collective-permute-start(bf16[128,1408]{1,0:T(8,128)(2,1)S(1)} %get-tuple-element.33), channel_id=1, source_target_pairs={{0,2},{1,3},{2,4},{3,5},{4,6},{5,7},{6,0},{7,1},{8,10},{9,11},{10,... | collective-permute-start | bytes 1081352 | tf_op jit(solution)/shard_map/ppermute | solution.py:35
  134.1 27.8 %collective-permute-start.13 = (bf16[128,4096]{1,0:T(8,128)(2,1)S(1)}, bf16[128,4096]{1,0:T(8,128)(2,1)S(1)}, u32[]{:S(2)}, u32[]{:S(2)}) collective-permute-start(bf16[128,4096]{1,0:T(8,128)(2,1)S(1)} %pad_maximum_fusion.5), channel_id=1, source_target_pairs={{0,6},{1,7},{2,0},{3,1},{4,2},{5,3},{6,4},{7,5},{8,14},{9,15},{10,... | collective-permute-start | bytes 3145736 | tf_op jit(solution)/shard_map/ppermute | solution.py:35
  139.2 27.1 %collective-permute-start.15 = (bf16[128,4096]{1,0:T(8,128)(2,1)S(1)}, bf16[128,4096]{1,0:T(8,128)(2,1)S(1)}, u32[]{:S(2)}, u32[]{:S(2)}) collective-permute-start(bf16[128,4096]{1,0:T(8,128)(2,1)S(1)} %pad_maximum_fusion.6), channel_id=1, source_target_pairs={{0,2},{1,3},{2,4},{3,5},{4,6},{5,7},{6,0},{7,1},{8,10},{9,11},{10,... | collective-permute-start | bytes 3145736 | tf_op jit(solution)/shard_map/ppermute | solution.py:35
  140.3 180.9 %collective-permute-start.11 = (bf16[128,4096]{1,0:T(8,128)(2,1)}, bf16[128,4096]{1,0:T(8,128)(2,1)}, u32[]{:S(2)}, u32[]{:S(2)}) collective-permute-start(bf16[128,4096]{1,0:T(8,128)(2,1)} %pad_maximum_fusion.4), channel_id=1, source_target_pairs={{0,1},{1,0},{2,3},{3,2},{4,5},{5,4},{6,7},{7,6},{8,9},{9,8},{10,11... | collective-permute-start | bytes 3145736 | tf_op jit(solution)/shard_map/ppermute | solution.py:35
  143.3 33.8 %collective-permute-start.21 = (bf16[128,4096]{1,0:T(8,128)(2,1)S(1)}, bf16[128,4096]{1,0:T(8,128)(2,1)S(1)}, u32[]{:S(2)}, u32[]{:S(2)}) collective-permute-start(bf16[128,4096]{1,0:T(8,128)(2,1)S(1)} %pad_maximum_fusion.7), channel_id=1, source_target_pairs={{0,6},{1,7},{2,0},{3,1},{4,2},{5,3},{6,4},{7,5},{8,14},{9,15},{10,... | collective-permute-start | bytes 3145736 | tf_op jit(solution)/shard_map/ppermute | solution.py:35
  148.0 36.5 %collective-permute-start.22 = (bf16[128,4096]{1,0:T(8,128)(2,1)S(1)}, bf16[128,4096]{1,0:T(8,128)(2,1)S(1)}, u32[]{:S(2)}, u32[]{:S(2)}) collective-permute-start(bf16[128,4096]{1,0:T(8,128)(2,1)S(1)} %pad_maximum_fusion.8), channel_id=1, source_target_pairs={{0,2},{1,3},{2,4},{3,5},{4,6},{5,7},{6,0},{7,1},{8,10},{9,11},{10,... | collective-permute-start | bytes 3145736 | tf_op jit(solution)/shard_map/ppermute | solution.py:35
  161.9 19.8 %collective-permute-start.23 = (bf16[128,4096]{1,0:T(8,128)(2,1)S(1)}, bf16[128,4096]{1,0:T(8,128)(2,1)S(1)}, u32[]{:S(2)}, u32[]{:S(2)}) collective-permute-start(bf16[128,4096]{1,0:T(8,128)(2,1)S(1)} %pad_maximum_fusion.9), channel_id=1, source_target_pairs={{0,1},{1,0},{2,3},{3,2},{4,5},{5,4},{6,7},{7,6},{8,9},{9,8},{10,11... | collective-permute-start | bytes 3145736 | tf_op jit(solution)/shard_map/ppermute | solution.py:35
  181.8 11.2 %collective-permute-start.25 = (bf16[128,1408]{1,0:T(8,128)(2,1)S(1)}, bf16[128,1408]{1,0:T(8,128)(2,1)S(1)}, u32[]{:S(2)}, u32[]{:S(2)}) collective-permute-start(bf16[128,1408]{1,0:T(8,128)(2,1)S(1)} %pad_maximum_fusion.13), channel_id=1, source_target_pairs={{0,6},{1,7},{2,0},{3,1},{4,2},{5,3},{6,4},{7,5},{8,14},{9,15},{10,... | collective-permute-start | bytes 1081352 | tf_op jit(solution)/shard_map/ppermute | solution.py:35
  184.6 8.4 %collective-permute-start.26 = (bf16[128,1280]{1,0:T(8,128)(2,1)S(1)}, bf16[128,1280]{1,0:T(8,128)(2,1)S(1)}, u32[]{:S(2)}, u32[]{:S(2)}) collective-permute-start(bf16[128,1280]{1,0:T(8,128)(2,1)S(1)} %pad_maximum_fusion.17), channel_id=1, source_target_pairs={{0,2},{1,3},{2,4},{3,5},{4,6},{5,7},{6,0},{7,1},{8,10},{9,11},{10,... | collective-permute-start | bytes 983048 | tf_op jit(solution)/shard_map/ppermute | solution.py:35
  184.8 8.2 %collective-permute-start.24 = (bf16[128,1408]{1,0:T(8,128)(2,1)S(1)}, bf16[128,1408]{1,0:T(8,128)(2,1)S(1)}, u32[]{:S(2)}, u32[]{:S(2)}) collective-permute-start(bf16[128,1408]{1,0:T(8,128)(2,1)S(1)} %pad_maximum_fusion.14), channel_id=1, source_target_pairs={{0,1},{1,0},{2,3},{3,2},{4,5},{5,4},{6,7},{7,6},{8,9},{9,8},{10,11... | collective-permute-start | bytes 1081352 | tf_op jit(solution)/shard_map/ppermute | solution.py:35
  211.2 15.6 %slice-start.8 = ((s8[8388608]{0:T(1024)(128)(4,1)}), s8[4194304]{0:T(1024)(128)(4,1)S(1)}, s32[]{:S(2)}) async-start(s8[8388608]{0:T(1024)(128)(4,1)} %bitcast.184), calls=%async_computation.10 | async-start | bytes 8388608
  272.6 20.3 %copy-start.9 = (bf16[128,1280]{1,0:T(8,128)(2,1)S(1)}, bf16[128,1280]{1,0:T(8,128)(2,1)}, u32[]{:S(2)}) copy-start(bf16[128,1280]{1,0:T(8,128)(2,1)} %get-tuple-element.29) | copy-start | bytes 983044
  273.5 11.0 %collective-permute-start.28 = (bf16[128,1280]{1,0:T(8,128)(2,1)S(1)}, bf16[128,1280]{1,0:T(8,128)(2,1)S(1)}, u32[]{:S(2)}, u32[]{:S(2)}) collective-permute-start(bf16[128,1280]{1,0:T(8,128)(2,1)S(1)} %copy-done.17), channel_id=1, source_target_pairs={{0,6},{1,7},{2,0},{3,1},{4,2},{5,3},{6,4},{7,5},{8,14},{9,15},{10,... | collective-permute-start | bytes 983048 | tf_op jit(solution)/shard_map/ppermute | solution.py:35
  277.7 11.4 %collective-permute-start.30 = (bf16[128,1408]{1,0:T(8,128)(2,1)S(1)}, bf16[128,1408]{1,0:T(8,128)(2,1)S(1)}, u32[]{:S(2)}, u32[]{:S(2)}) collective-permute-start(bf16[128,1408]{1,0:T(8,128)(2,1)S(1)} %get-tuple-element.27), channel_id=1, source_target_pairs={{0,1},{1,0},{2,3},{3,2},{4,5},{5,4},{6,7},{7,6},{8,9},{9,8},{10,11... | collective-permute-start | bytes 1081352 | tf_op jit(solution)/shard_map/ppermute | solution.py:35
  278.8 12.5 %collective-permute-start.27 = (bf16[128,1408]{1,0:T(8,128)(2,1)S(1)}, bf16[128,1408]{1,0:T(8,128)(2,1)S(1)}, u32[]{:S(2)}, u32[]{:S(2)}) collective-permute-start(bf16[128,1408]{1,0:T(8,128)(2,1)S(1)} %get-tuple-element.28), channel_id=1, source_target_pairs={{0,2},{1,3},{2,4},{3,5},{4,6},{5,7},{6,0},{7,1},{8,10},{9,11},{10,... | collective-permute-start | bytes 1081352 | tf_op jit(solution)/shard_map/ppermute | solution.py:35
  285.8 30.4 %slice-start = ((s8[16777216]{0:T(1024)(128)(4,1)}), s8[4194304]{0:T(1024)(128)(4,1)S(1)}, s32[]{:S(2)}) async-start(s8[16777216]{0:T(1024)(128)(4,1)} %bitcast.167), calls=%async_computation.2 | async-start | bytes 8388608
  285.8 41.1 %slice-start.4 = ((s8[16777216]{0:T(1024)(128)(4,1)}), s8[4194304]{0:T(1024)(128)(4,1)S(1)}, s32[]{:S(2)}) async-start(s8[16777216]{0:T(1024)(128)(4,1)} %bitcast.169), calls=%async_computation.6 | async-start | bytes 8388608
  292.8 23.3 %slice-start.1 = ((s8[16777216]{0:T(1024)(128)(4,1)}), s8[4194304]{0:T(1024)(128)(4,1)S(1)}, s32[]{:S(2)}) async-start(s8[16777216]{0:T(1024)(128)(4,1)} %bitcast.167), calls=%async_computation.3 | async-start | bytes 8388608
  293.2 33.7 %slice-start.5 = ((s8[16777216]{0:T(1024)(128)(4,1)}), s8[4194304]{0:T(1024)(128)(4,1)S(1)}, s32[]{:S(2)}) async-start(s8[16777216]{0:T(1024)(128)(4,1)} %bitcast.169), calls=%async_computation.7 | async-start | bytes 8388608
  293.3 18.6 %collective-permute-start.31 = (bf16[128,4096]{1,0:T(8,128)(2,1)S(1)}, bf16[128,4096]{1,0:T(8,128)(2,1)S(1)}, u32[]{:S(2)}, u32[]{:S(2)}) collective-permute-start(bf16[128,4096]{1,0:T(8,128)(2,1)S(1)} %pad_maximum_fusion.11), channel_id=1, source_target_pairs={{0,6},{1,7},{2,0},{3,1},{4,2},{5,3},{6,4},{7,5},{8,14},{9,15},{10,... | collective-permute-start | bytes 3145736 | tf_op jit(solution)/shard_map/ppermute | solution.py:35
  294.0 22.2 %slice-start.2 = ((s8[16777216]{0:T(1024)(128)(4,1)}), s8[4194304]{0:T(1024)(128)(4,1)S(1)}, s32[]{:S(2)}) async-start(s8[16777216]{0:T(1024)(128)(4,1)} %bitcast.167), calls=%async_computation.4 | async-start | bytes 8388608
  294.1 18.9 %collective-permute-start.33 = (bf16[128,4096]{1,0:T(8,128)(2,1)S(1)}, bf16[128,4096]{1,0:T(8,128)(2,1)S(1)}, u32[]{:S(2)}, u32[]{:S(2)}) collective-permute-start(bf16[128,4096]{1,0:T(8,128)(2,1)S(1)} %pad_maximum_fusion.12), channel_id=1, source_target_pairs={{0,2},{1,3},{2,4},{3,5},{4,6},{5,7},{6,0},{7,1},{8,10},{9,11},{10,... | collective-permute-start | bytes 3145736 | tf_op jit(solution)/shard_map/ppermute | solution.py:35
  295.8 18.8 %collective-permute-start.29 = (bf16[128,4096]{1,0:T(8,128)(2,1)S(1)}, bf16[128,4096]{1,0:T(8,128)(2,1)S(1)}, u32[]{:S(2)}, u32[]{:S(2)}) collective-permute-start(bf16[128,4096]{1,0:T(8,128)(2,1)S(1)} %pad_maximum_fusion.10), channel_id=1, source_target_pairs={{0,1},{1,0},{2,3},{3,2},{4,5},{5,4},{6,7},{7,6},{8,9},{9,8},{10,11... | collective-permute-start | bytes 3145736 | tf_op jit(solution)/shard_map/ppermute | solution.py:35
  313.0 13.9 %slice-start.6 = ((s8[16777216]{0:T(1024)(128)(4,1)}), s8[4194304]{0:T(1024)(128)(4,1)S(1)}, s32[]{:S(2)}) async-start(s8[16777216]{0:T(1024)(128)(4,1)} %bitcast.169), calls=%async_computation.8 | async-start | bytes 8388608
  316.5 10.3 %slice-start.7 = ((s8[16777216]{0:T(1024)(128)(4,1)}), s8[4194304]{0:T(1024)(128)(4,1)S(1)}, s32[]{:S(2)}) async-start(s8[16777216]{0:T(1024)(128)(4,1)} %bitcast.169), calls=%async_computation.9 | async-start | bytes 8388608
  316.5 10.3 %copy-start.4 = (f32[64,4096]{1,0:T(8,128)S(1)}, f32[64,4096]{1,0:T(8,128)}, u32[]{:S(2)}) copy-start(f32[64,4096]{1,0:T(8,128)} %get-tuple-element.66) | copy-start | bytes 3145732
  316.5 10.4 %copy-start.5 = (f32[64,4096]{1,0:T(8,128)S(1)}, f32[64,4096]{1,0:T(8,128)}, u32[]{:S(2)}) copy-start(f32[64,4096]{1,0:T(8,128)} %get-tuple-element.67) | copy-start | bytes 3145732
  321.0 21.0 %collective-permute-start.32 = (bf16[128,4096]{1,0:T(8,128)(2,1)}, bf16[128,4096]{1,0:T(8,128)(2,1)}, u32[]{:S(2)}, u32[]{:S(2)}) collective-permute-start(bf16[128,4096]{1,0:T(8,128)(2,1)} %get-tuple-element.16), channel_id=1, source_target_pairs={{0,6},{1,7},{2,0},{3,1},{4,2},{5,3},{6,4},{7,5},{8,14},{9,15},{10,... | collective-permute-start | bytes 3145736 | tf_op jit(solution)/shard_map/ppermute | solution.py:35
  324.2 32.5 %collective-permute-start.35 = (bf16[128,4096]{1,0:T(8,128)(2,1)}, bf16[128,4096]{1,0:T(8,128)(2,1)}, u32[]{:S(2)}, u32[]{:S(2)}) collective-permute-start(bf16[128,4096]{1,0:T(8,128)(2,1)} %get-tuple-element.17), channel_id=1, source_target_pairs={{0,1},{1,0},{2,3},{3,2},{4,5},{5,4},{6,7},{7,6},{8,9},{9,8},{10,11... | collective-permute-start | bytes 3145736 | tf_op jit(solution)/shard_map/ppermute | solution.py:35
  326.3 30.4 %collective-permute-start.34 = (bf16[128,4096]{1,0:T(8,128)(2,1)}, bf16[128,4096]{1,0:T(8,128)(2,1)}, u32[]{:S(2)}, u32[]{:S(2)}) collective-permute-start(bf16[128,4096]{1,0:T(8,128)(2,1)} %get-tuple-element.18), channel_id=1, source_target_pairs={{0,2},{1,3},{2,4},{3,5},{4,6},{5,7},{6,0},{7,1},{8,10},{9,11},{10,... | collective-permute-start | bytes 3145736 | tf_op jit(solution)/shard_map/ppermute | solution.py:35
  326.9 29.8 %copy-start.3 = (bf16[1,128,4096]{2,1,0:T(8,128)(2,1)S(1)}, bf16[1,128,4096]{2,1,0:T(8,128)(2,1)}, u32[]{:S(2)}) copy-start(bf16[1,128,4096]{2,1,0:T(8,128)(2,1)} %param.8) | copy-start | bytes 3145732
  326.9 29.8 %copy-start.19 = (f32[4096]{0:T(1024)S(1)}, f32[4096]{0:T(1024)}, u32[]{:S(2)}) copy-start(f32[4096]{0:T(1024)} %copy-done.18) | copy-start | bytes 49156
  326.9 29.8 %copy-start.25 = (f32[128]{0:T(128)S(1)}, f32[128]{0:T(128)}, u32[]{:S(2)}) copy-start(f32[128]{0:T(128)} %copy-done.24) | copy-start | bytes 1540
  330.7 57.5 %collective-permute-start.14 = (bf16[128,4096]{1,0:T(8,128)(2,1)}, bf16[128,4096]{1,0:T(8,128)(2,1)}, u32[]{:S(2)}, u32[]{:S(2)}) collective-permute-start(bf16[128,4096]{1,0:T(8,128)(2,1)} %get-tuple-element.21), channel_id=1, source_target_pairs={{0,6},{1,7},{2,0},{3,1},{4,2},{5,3},{6,4},{7,5},{8,14},{9,15},{10,... | collective-permute-start | bytes 3145736 | tf_op jit(solution)/shard_map/ppermute | solution.py:35
  333.4 54.9 %collective-permute-start.17 = (bf16[128,4096]{1,0:T(8,128)(2,1)}, bf16[128,4096]{1,0:T(8,128)(2,1)}, u32[]{:S(2)}, u32[]{:S(2)}) collective-permute-start(bf16[128,4096]{1,0:T(8,128)(2,1)} %get-tuple-element.22), channel_id=1, source_target_pairs={{0,1},{1,0},{2,3},{3,2},{4,5},{5,4},{6,7},{7,6},{8,9},{9,8},{10,11... | collective-permute-start | bytes 3145736 | tf_op jit(solution)/shard_map/ppermute | solution.py:35
  342.0 46.2 %collective-permute-start.16 = (bf16[128,4096]{1,0:T(8,128)(2,1)}, bf16[128,4096]{1,0:T(8,128)(2,1)}, u32[]{:S(2)}, u32[]{:S(2)}) collective-permute-start(bf16[128,4096]{1,0:T(8,128)(2,1)} %get-tuple-element.23), channel_id=1, source_target_pairs={{0,2},{1,3},{2,4},{3,5},{4,6},{5,7},{6,0},{7,1},{8,10},{9,11},{10,... | collective-permute-start | bytes 3145736 | tf_op jit(solution)/shard_map/ppermute | solution.py:35
  360.7 1.2 collective-permute-start.36
  361.9 4.0 collective-permute-start.37
  365.9 31.8 %copy-start.1 = (bf16[256,4096]{1,0:T(8,128)(2,1)S(1)}, bf16[256,4096]{1,0:T(8,128)(2,1)}, u32[]{:S(2)}) copy-start(bf16[256,4096]{1,0:T(8,128)(2,1)} %param.13) | copy-start | bytes 6291460
  365.9 5.2 %collective-permute-start.38 = (f32[4096]{0:T(1024)S(1)}, f32[4096]{0:T(1024)S(1)}, u32[]{:S(2)}, u32[]{:S(2)}) collective-permute-start(f32[4096]{0:T(1024)S(1)} %add.230), channel_id=1, source_target_pairs={{0,32},{8,40},{16,48},{24,56},{32,0},{40,8},{48,16},{56,24},{64,96... | collective-permute-start | bytes 49160 | tf_op jit(solution)/shard_map/ppermute | solution.py:106
  371.1 8.5 %collective-permute-start.39 = (f32[4096]{0:T(1024)S(1)}, f32[4096]{0:T(1024)S(1)}, u32[]{:S(2)}, u32[]{:S(2)}) collective-permute-start(f32[4096]{0:T(1024)S(1)} %add.231), channel_id=1, source_target_pairs={{0,64},{8,72},{16,80},{24,88},{32,96},{40,104},{48,112},{56,120},{... | collective-permute-start | bytes 49160 | tf_op jit(solution)/shard_map/ppermute | solution.py:106
  379.7 3.7 collective-permute-start.40
  383.4 3.7 collective-permute-start.41
  387.2 6.7 %collective-permute-start.42 = (f32[4096]{0:T(1024)S(1)}, f32[4096]{0:T(1024)S(1)}, u32[]{:S(2)}, u32[]{:S(2)}) collective-permute-start(f32[4096]{0:T(1024)S(1)} %add.234), channel_id=1, source_target_pairs={{0,4},{1,5},{2,6},{3,7},{4,0},{5,1},{6,2},{7,3},{8,12},{9,13},{10,... | collective-permute-start | bytes 49160 | tf_op jit(solution)/shard_map/ppermute | solution.py:35
  (18 other events, 84.7 us)
Sparse Core Ops, SparseCore 0:
  272.7 107.9 reduce-scatter.1
